TPU v7x, 32 devices: a whole 2x2x4 slice. The times are simulated.
32 devices in a mesh: shot: 8 (over z, y), rcv: 4 (over x, core).
Axes of the slice: x: 2, y: 2, z: 4, core: 2. Of those that a mesh axis runs over, the one named last changes fastest.
Arguments:
- records: bfloat16 [1, 2, 1024, 8192], P(None, None, 'shot', 'rcv'), may hold values from -6 to 6
- aperture: int32 [1024, 2], P('shot'), may hold values from 0 to 3, all different within a row
- block_owner: int32 [4], replicated, may hold values from 0 to 7, as said below
- block_receivers: int32 [4, 128], replicated, may hold values from 0 to 8191, as said below
Outputs:
- multiples: bfloat16 [1, 2, 1024, 8192], P(None, None, 'shot', 'rcv')
Inputs may be any that keep to these rules, and one draw needn't show every extreme that they name: `block_owner`: distinct indices. `block_receivers`: distinct receivers.
All inputs are finite; a program needn't handle non-finite values.
Results may differ from a plain program's by a relative error of at most 0.001.
Values may be sent and summed in bfloat16 or wider, within the bound.
No kernel may reach another device: no remote copies, remote signals or barrier semaphores. Data moves between devices by JAX's collectives and lax.ppermute only.
A program may use at most 128 MiB of HBM per device.

v0:
```python
import jax
import jax.numpy as jnp
from jax import lax
from jax.sharding import PartitionSpec as P

APER = 2
BLOCK = 128


def broadcast(value, axis, source):
    kept = jnp.where(lax.axis_index(axis) == source, value, 0).astype(value.dtype)
    return lax.psum(kept, axis)


def complex_terms(block_portion, distant_offset):
    real_component = jnp.einsum(
        "uze,uew->uzw",
        block_portion[:, 0],
        distant_offset[:, 0],
        preferred_element_type=jnp.float32,
    ) - jnp.einsum(
        "uze,uew->uzw",
        block_portion[:, 1],
        distant_offset[:, 1],
        preferred_element_type=jnp.float32,
    )
    imag_part = jnp.einsum(
        "uze,uew->uzw",
        block_portion[:, 0],
        distant_offset[:, 1],
        preferred_element_type=jnp.float32,
    ) + jnp.einsum(
        "uze,uew->uzw",
        block_portion[:, 1],
        distant_offset[:, 0],
        preferred_element_type=jnp.float32,
    )
    return (real_component, imag_part)


def per_device(records, aperture, block_owner, block_receivers):
    freqs, parts, shots_here, rcv_here = records.shape
    nblocks, block_extent = block_receivers.shape
    first_rcv = lax.axis_index("rcv") * rcv_here
    requested_rows = block_receivers.reshape(1, -1)
    column_ids = first_rcv + lax.broadcasted_iota(jnp.int32, (rcv_here, 1), 0)
    selector = (column_ids == requested_rows).astype(jnp.bfloat16)
    local_cols = jnp.einsum("fcsr,rx->fcsx", records, selector, preferred_element_type=jnp.float32)
    near = lax.psum(local_cols.astype(jnp.bfloat16), "rcv")
    blocks = lax.broadcasted_iota(jnp.int32, (1, 1, nblocks), 2)
    use = jnp.any(aperture[:, :, None] == blocks, axis=1).astype(jnp.bfloat16)
    masked = (
        near.reshape(freqs, parts, shots_here, nblocks, block_extent) * use[None, None, :, :, None]
    )
    masked = masked.reshape(freqs, parts, shots_here, nblocks * block_extent)

    def fetch(block):
        return broadcast(records, "shot", block_owner[block])

    real_total = jnp.zeros((freqs, shots_here, rcv_here), jnp.float32)
    imaginary_total = jnp.zeros((freqs, shots_here, rcv_here), jnp.float32)
    gathered_rows = [fetch(block) for block in range(nblocks)]
    for block in range(nblocks):
        block_portion = masked[:, :, :, block * block_extent : (block + 1) * block_extent]
        real_component, imag_part = complex_terms(block_portion, gathered_rows[block])
        real_total = real_total + real_component
        imaginary_total = imaginary_total + imag_part
    factor = (2.0 * APER * BLOCK) ** (-0.5)
    return (jnp.stack([real_total, imaginary_total], axis=1) * factor).astype(jnp.bfloat16)


def solution(mesh):
    placed = (P(None, None, "shot", "rcv"), P("shot", None), P(), P())
    return jax.shard_map(
        per_device,
        mesh=mesh,
        in_specs=placed,
        out_specs=P(None, None, "shot", "rcv"),
        check_vma=False,
    )
```

profile of v0, /device:TPU:0, one launch (start us, length us, event | category | flops | bytes accessed | tf_op | source)
XLA Modules:
  0.0 222.4 jit_solution(10446118807844659125)
XLA Ops:
  6.5 0.0 all-reduce.4.cloned.1.call-start
  6.5 0.0 copy-start.5
  6.5 0.0 copy-start.4
  6.6 2.8 %fusion.17 = bf16[1,2,128,512]{2,3,1,0:T(8,128)(2,1)} fusion(s32[2048]{0:T(1024)S(1)} %iota_add_fusion, s32[512]{0:T(512)} %bitcast.89, bf16[1,2,128,2048]{3,2,1,0:T(8,128)(2,1)} %param.4), kind=kOutput, calls=%fused_computation.24 | convolution fusion | flops 538050560 | bytes 1320960 | tf_op jit(solution)/shard_map/fcsr,rx->fcsx/dot_general | solution.py:48
  9.4 0.0 all-reduce.4.cloned.1.call-update
  9.4 0.0 all-reduce.6.cloned.1.call-start
  9.4 0.0 copy-done.5
  9.4 0.7 fusion.30
  12.7 0.0 copy-done.4
  12.7 2.1 broadcast_select_fusion
  14.8 0.0 copy-start.6
  14.8 0.0 all-reduce.6.cloned.1.call-update
  14.8 0.7 copy-done.6
  15.5 29.2 %all-reduce.4.cloned.1.call-done = bf16[1,2,128,512]{2,3,1,0:T(8,128)(2,1)} async-done(((bf16[1,2,128,512]{2,3,1,0:T(8,128)(2,1)}), bf16[1,2,128,512]{2,3,1,0:T(8,128)(2,1)}) %all-reduce.4.cloned.1.call-update) | async-done | bytes 262160 | tf_op jit(solution)/shard_map/psum | solution.py:49
  44.7 1.0 broadcast_multiply_fusion
  45.7 159.6 %all-reduce.6.cloned.1.call-done = (bf16[1,2,128,2048]{3,2,1,0:T(8,128)(2,1)}, bf16[1,2,128,2048]{3,2,1,0:T(8,128)(2,1)}, bf16[1,2,128,2048]{3,2,1,0:T(8,128)(2,1)}, bf16[1,2,128,2048]{3,2,1,0:T(8,128)(2,1)}) async-done(((bf16[1,2,128,2048]{3,2,1,0:T(8,128)(2,1)}, bf16[1,2,128,2048]{3,2,1,0:T(8,128)(2,1)}, bf16[1,2,128,2048]{3,2,1,0:T(8,128)(2,1)}, bf16[1,2,128,2048]{3,2,1,0:T(8,128)(2,1)}), ...) | async-done | bytes 4194320 | tf_op jit(solution)/shard_map/psum | solution.py:12
  205.3 0.0 copy-start.3
  205.3 1.4 fusion.21
  206.7 0.0 copy-done.3
  206.7 0.0 copy-start.2
  206.7 0.3 fusion.22
  207.1 0.9 copy-done.2
  208.0 0.3 fusion.23
  208.3 0.0 copy-start.1
  208.3 0.3 fusion.24
  208.6 0.9 copy-done.1
  209.5 0.3 fusion.25
  209.8 0.0 copy-start
  209.9 0.3 fusion.26
  210.2 0.9 copy-done
  211.1 0.3 fusion.27
  211.4 0.3 fusion.28
  211.7 0.3 convolution_subtract_fusion.3
  212.0 0.3 convolution_add_fusion.3
  212.4 0.3 fusion.10
  212.7 0.3 fusion.9
  213.1 0.3 fusion.8
  213.4 0.3 fusion.6
  213.7 0.3 fusion.5
  214.1 0.3 fusion.4
  214.4 1.2 fusion.11
  (4 shorter events, 0.0 us)
Async XLA Ops:
  6.5 38.2 %all-reduce.4.cloned.1.call-start = ((), (), s32[]{:S(2)}) async-start(), calls=%async_computation | async-start | bytes 524288 | tf_op jit(solution)/shard_map/psum | solution.py:49
  6.5 2.9 %copy-start.5 = (s32[4]{0:T(128)S(1)}, s32[4]{0:T(128)}, u32[]{:S(2)}) copy-start(s32[4]{0:T(128)} %param.6) | copy-start | bytes 52
  6.5 6.2 %copy-start.4 = (bf16[1,2,128,2048]{3,2,1,0:T(8,128)(2,1)S(1)}, bf16[1,2,128,2048]{3,2,1,0:T(8,128)(2,1)}, u32[]{:S(2)}) copy-start(bf16[1,2,128,2048]{3,2,1,0:T(8,128)(2,1)} %param.4) | copy-start | bytes 3145732
  9.4 195.9 %all-reduce.6.cloned.1.call-start = ((), (), s32[]{:S(2)}) async-start(), calls=%async_computation.1 | async-start | bytes 8388608 | tf_op jit(solution)/shard_map/psum | solution.py:12
  14.8 0.7 copy-start.6
  205.3 1.5 copy-start.3
  206.7 1.2 copy-start.2
  208.3 1.2 copy-start.1
  209.8 1.2 copy-start
Sparse Core Ops, SparseCore 0:
  9.7 34.9 all-reduce.3
  48.7 156.4 all-reduce.5
where the time goes:
time: 223 us; the launch traced here: 222 us
  waiting for transfers between devices  189 us (85%)
  between operations  16.1 us (7%)
  matrix products  9.14 us (4%)
  other arithmetic  4.27 us (2%)
  local copies, waits for them, and re-layouts  4.04 us (2%)
    psum x1, waiting for transfers between devices, broadcast(): return lax.psum(kept, axis)  160 us
    psum x1, waiting for transfers between devices, per_device(): near = lax.psum(local_cols.astype(jnp.bfloat16), 'rcv')  29.2 us
  transfers between devices with their start and end apart: 2, of which 2 were waited for; matrix products, arithmetic and copies ran while one was open for 2% of the time, Pallas kernels for 0%

commit v1 on v0

v1 whole, which is shorter than its diff:
```python
import jax
import jax.numpy as jnp
from jax import lax
from jax.sharding import PartitionSpec as P

APER = 2
BLOCK = 128


def ring_order(n):
    if n % 2:
        return list(range(n))
    return list(range(0, n, 2)) + list(range(n - 1, 0, -2))


def local_columns(records, block_receivers):
    rcv_here = records.shape[3]
    first_rcv = lax.axis_index("rcv") * rcv_here
    requested = block_receivers.reshape(1, -1)
    column_ids = first_rcv + lax.broadcasted_iota(jnp.int32, (rcv_here, 1), 0)
    selector = (column_ids == requested).astype(jnp.bfloat16)
    picked = jnp.einsum("fcsr,rx->fcsx", records, selector, preferred_element_type=jnp.float32)
    return picked.astype(jnp.bfloat16)


def gather_near(picked, n_rcv):
    total = picked.astype(jnp.float32)
    for k in range(1, n_rcv):
        moved = lax.ppermute(picked, "rcv", [(i, (i + k) % n_rcv) for i in range(n_rcv)])
        total = total + moved.astype(jnp.float32)
    return total.astype(jnp.bfloat16)


def piece_product(lhs, piece):
    nblk, freqs, parts, extent, width = piece.shape
    rhs = piece.transpose(1, 2, 0, 3, 4).reshape(freqs, parts * nblk * extent, width)
    return jnp.einsum("fsk,fkw->fsw", lhs, rhs, preferred_element_type=jnp.float32)


def per_device(records, aperture, block_owner, block_receivers, n_shot, n_rcv):
    freqs, parts, shots_here, rcv_here = records.shape
    nblocks, block_extent = block_receivers.shape
    width = rcv_here // n_shot

    picked = local_columns(records, block_receivers)
    near = gather_near(picked, n_rcv)
    blocks = lax.broadcasted_iota(jnp.int32, (1, 1, nblocks), 2)
    use = jnp.any(aperture[:, :, None] == blocks, axis=1).astype(jnp.bfloat16)
    masked = near.reshape(freqs, parts, shots_here, nblocks, block_extent) * use[None, None, :, :, None]
    masked = masked.reshape(freqs, parts, shots_here, nblocks * block_extent)
    nr, ni = masked[:, 0], masked[:, 1]
    lhs = jnp.concatenate(
        [jnp.concatenate([nr, -ni], axis=2), jnp.concatenate([ni, nr], axis=2)], axis=1
    )

    pieces = records.reshape(freqs, parts, shots_here, n_shot, width).transpose(3, 0, 1, 2, 4)
    pieces = lax.all_to_all(pieces, "shot", 0, 0, tiled=True)
    mine = jnp.take(pieces, block_owner, axis=0)

    order = ring_order(n_shot)
    where = [0] * n_shot
    for k, d in enumerate(order):
        where[d] = k
    order_arr = jnp.array(order, jnp.int32)
    me = lax.axis_index("shot")
    pos = jnp.array(where, jnp.int32)[me]
    forward = [(order[k], order[(k + 1) % n_shot]) for k in range(n_shot)]
    backward = [(order[k], order[(k - 1) % n_shot]) for k in range(n_shot)]
    n_fwd = n_shot // 2
    n_bwd = n_shot - 1 - n_fwd

    outs = [piece_product(lhs, mine)]
    came_from = [me]
    fwd, bwd = mine, mine
    for t in range(1, max(n_fwd, n_bwd) + 1):
        if t <= n_fwd:
            fwd = lax.ppermute(fwd, "shot", forward)
            outs.append(piece_product(lhs, fwd))
            came_from.append(order_arr[(pos - t) % n_shot])
        if t <= n_bwd:
            bwd = lax.ppermute(bwd, "shot", backward)
            outs.append(piece_product(lhs, bwd))
            came_from.append(order_arr[(pos + t) % n_shot])
    came_from = jnp.stack(came_from)
    arrival = jnp.zeros((n_shot,), jnp.int32).at[came_from].set(jnp.arange(n_shot, dtype=jnp.int32))
    stacked = jnp.take(jnp.stack(outs), arrival, axis=0)
    factor = (2.0 * APER * BLOCK) ** (-0.5)
    total = (stacked * factor).astype(jnp.bfloat16)
    total = total.reshape(n_shot, freqs, parts, shots_here, width).transpose(1, 2, 3, 0, 4)
    return total.reshape(freqs, parts, shots_here, rcv_here)


def solution(mesh):
    n_shot = mesh.shape["shot"]
    n_rcv = mesh.shape["rcv"]
    placed = (P(None, None, "shot", "rcv"), P("shot", None), P(), P())

    def body(records, aperture, block_owner, block_receivers):
        return per_device(records, aperture, block_owner, block_receivers, n_shot, n_rcv)

    return jax.shard_map(
        body,
        mesh=mesh,
        in_specs=placed,
        out_specs=P(None, None, "shot", "rcv"),
        check_vma=False,
    )
```

time: 223 us -> 90.7 us (0.41)
  waiting for transfers between devices: 189 us -> 51.3 us
  starting transfers between devices: 0.04 us -> 15.5 us
  between operations: 16.1 us -> 4.34 us
  local copies, waits for them, and re-layouts: 4.04 us -> 14.8 us
  matrix products: 9.14 us -> 3.53 us
  other arithmetic: 4.27 us -> 0.81 us
    psum x2 -> x0, waiting for transfers between devices: 189 us -> none  [the longest x1 160 us: broadcast(): return lax.psum(kept, axis)]
    ppermute x0 -> x10, waiting for transfers between devices: none -> 38.5 us  [the longest x4 37.5 us: per_device(): fwd = lax.ppermute(fwd, 'shot', forward)]
    all_to_all x0 -> x1, waiting for transfers between devices: none -> 12.8 us  [per_device(): pieces = lax.all_to_all(pieces, 'shot', 0, 0, tiled=True)]
    ppermute x0 -> x10, starting transfers between devices: none -> 8.23 us  [the longest x3 5.64 us: per_device(): bwd = lax.ppermute(bwd, 'shot', backward)]
    all_to_all x0 -> x1, starting transfers between devices: none -> 7.31 us  [per_device(): pieces = lax.all_to_all(pieces, 'shot', 0, 0, tiled=True)]
    dot_general x17 -> x9, matrix products: 9.14 us -> 3.53 us  [the longest x8 2.76 us: piece_product(): jnp.einsum('fsk,fkw->fsw', lhs, rhs, preferred_element_type=jnp.float32)]
    another operation x0 -> x1, local copies, waits for them, and re-layouts: none -> 4.45 us  [per_device(): came_from = jnp.stack(came_from)]
    gather x0 -> x2, local copies, waits for them, and re-layouts: none -> 2.85 us  [the longest x1 2.27 us: per_device(): stacked = jnp.take(jnp.stack(outs), arrival, axis=0)]
  transfers between devices with their start and end apart: 2 -> 11, of which waited for: 2 -> 7; matrix products, arithmetic and copies ran while one was open for 2% -> 12% of each run, Pallas kernels for 0% -> 0%
where the time goes in v1:
time: 90.7 us; the launch traced here: 90.4 us
  waiting for transfers between devices  51.3 us (57%)
  starting transfers between devices  15.5 us (17%)
  local copies, waits for them, and re-layouts  14.8 us (16%)
  between operations  4.34 us (5%)
  matrix products  3.53 us (4%)
    ppermute x4, waiting for transfers between devices, per_device(): fwd = lax.ppermute(fwd, 'shot', forward)  37.5 us
    all_to_all x1, waiting for transfers between devices, per_device(): pieces = lax.all_to_all(pieces, 'shot', 0, 0, tiled=True)  12.8 us
    all_to_all x1, starting transfers between devices, per_device(): pieces = lax.all_to_all(pieces, 'shot', 0, 0, tiled=True)  7.31 us
    ppermute x3, starting transfers between devices, per_device(): bwd = lax.ppermute(bwd, 'shot', backward)  5.64 us
    another operation x1, local copies, waits for them, and re-layouts, per_device(): came_from = jnp.stack(came_from)  4.45 us
    unnamed x15, local copies, waits for them, and re-layouts  2.97 us
    dot_general x8, matrix products, piece_product(): jnp.einsum('fsk,fkw->fsw', lhs, rhs, preferred_element_type=jnp.float32)  2.76 us
    gather x1, local copies, waits for them, and re-layouts, per_device(): stacked = jnp.take(jnp.stack(outs), arrival, axis=0)  2.27 us
  transfers between devices with their start and end apart: 11, of which 7 were waited for; matrix products, arithmetic and copies ran while one was open for 12% of the time, Pallas kernels for 0%

profile of v1, /device:TPU:0, one launch (start us, length us, event | category | flops | bytes accessed | tf_op | source)
XLA Modules:
  0.0 90.4 jit_solution(7061139052418597800)
XLA Ops:
  0.0 1.6 %copy.43 = bf16[1,2,128,2048]{2,3,1,0:T(8,128)(2,1)S(1)} copy(bf16[1,2,128,2048]{3,2,1,0:T(8,128)(2,1)} %param.6) | data formatting | bytes 2097152 | tf_op args[0]
  1.6 0.0 copy-start.1
  1.6 0.0 copy-start.3
  1.6 1.3 %copy.44 = bf16[8,1,2,128,256]{4,3,2,1,0:T(8,128)(2,1)} copy(bf16[8,1,2,128,256]{3,4,0,2,1:T(8,128)(2,1)S(1)} %bitcast.121) | data formatting | bytes 2097152 | tf_op jit(solution)/shard_map/transpose | solution.py:56
  3.0 7.3 %all-to-all-start = ((bf16[8,1,2,128,256]{4,3,2,1,0:T(8,128)(2,1)}), bf16[8,1,2,128,256]{4,3,2,1,0:T(8,128)(2,1)S(1)}, u32[]{:S(2)}, u32[]{:S(2)}) async-start(bf16[8,1,2,128,256]{4,3,2,1,0:T(8,128)(2,1)} %copy.44), calls=%async_computation | async-start | bytes 2097152 | tf_op jit(solution)/shard_map/all_to_all | solution.py:57
  10.3 0.0 copy-start.6
  10.3 0.0 copy-start.2
  10.3 0.0 copy-start.5
  10.3 0.0 copy-start.4
  10.3 0.0 copy-done.1
  10.3 0.0 copy-done.3
  10.3 0.8 fusion.16
  11.1 0.7 collective-permute-start.2
  11.8 0.9 %collective-permute-start.1 = (bf16[1,2,128,512]{2,3,1,0:T(8,128)(2,1)S(1)}, bf16[1,2,128,512]{2,3,1,0:T(8,128)(2,1)S(1)}, u32[]{:S(2)}, u32[]{:S(2)}) collective-permute-start(bf16[1,2,128,512]{2,3,1,0:T(8,128)(2,1)S(1)} %fusion.16), channel_id=1, source_target_pairs={{0,2},{1,3},{2,0},{3,1},{4,6},{5,7},{6,4},{7,5},{8,10},{9,11},{10,... | collective-permute-start | bytes 786440 | tf_op jit(solution)/shard_map/ppermute | solution.py:29
  12.7 0.2 collective-permute-start
  12.9 0.0 copy-done.6
  12.9 0.6 dynamic_slice.24
  17.4 0.0 copy-done.2
  17.4 0.7 fusion.27
  18.1 4.5 %stack.55 = s32[8,1]{0,1:T(1,128)S(1)} concatenate(s32[1,1]{0,1:T(1,128)} %bitcast, s32[1,1]{0,1:T(1,128)} %bitcast.2, s32[1,1]{0,1:T(1,128)} %bitcast.4, s32[1,1]{0,1:T(1,128)} %bitcast.6, s32[1,1]{0,1:T(1,128)} %bitcast.8, s32[1,1]{0,1:T(1,128)} %bitcast.10, s32[1,1]{0,1:T(1,128)} %bitcast.12, s32[1,1]{0,1:T(1,128)} %bitcast.14), dimensions={0} | concatenate | bytes 64 | tf_op jit(solution)/shard_map/stack | solution.py:84
  22.6 0.6 scatter_custom_fusion
  23.2 0.0 copy-done.5
  23.2 0.0 copy-done.4
  23.3 12.8 %all-to-all-done = bf16[8,1,2,128,256]{4,3,2,1,0:T(8,128)(2,1)S(1)} async-done(((bf16[8,1,2,128,256]{4,3,2,1,0:T(8,128)(2,1)}), bf16[8,1,2,128,256]{4,3,2,1,0:T(8,128)(2,1)S(1)}, u32[]{:S(2)}, u32[]{:S(2)}) %all-to-all-start) | async-done | bytes 1048608 | tf_op jit(solution)/shard_map/all_to_all | solution.py:57
  36.0 0.6 gather_fusion
  36.6 0.1 bitcast_select_fusion
  36.7 0.1 collective-permute-start.3
  36.8 2.1 %collective-permute-start.4 = (bf16[4,1,2,128,256]{4,3,2,0,1:T(8,128)(2,1)S(1)}, bf16[4,1,2,128,256]{4,3,2,0,1:T(8,128)(2,1)S(1)}, u32[]{:S(2)}, u32[]{:S(2)}) collective-permute-start(bf16[4,1,2,128,256]{4,3,2,0,1:T(8,128)(2,1)S(1)} %bitcast_select_fusion), channel_id=1, source_target_pairs={{0,4},{8,0},{16,8},{24,16},{28,24},{20,28},{12,20},{4,12},{1,5},{9... | collective-permute-start | bytes 1572872 | tf_op jit(solution)/shard_map/ppermute | solution.py:81
  38.9 0.0 collective-permute-done.2
  38.9 0.0 collective-permute-done.1
  38.9 0.0 collective-permute-done
  38.9 0.2 fusion.21
  39.1 10.3 %collective-permute-done.3 = bf16[4,1,2,128,256]{4,3,2,0,1:T(8,128)(2,1)S(1)} collective-permute-done((bf16[4,1,2,128,256]{4,3,2,0,1:T(8,128)(2,1)S(1)}, bf16[4,1,2,128,256]{4,3,2,0,1:T(8,128)(2,1)S(1)}, u32[]{:S(2)}, u32[]{:S(2)}) %collective-permute-start.3) | collective-permute-done | bytes 524320 | tf_op jit(solution)/shard_map/ppermute | solution.py:77
  49.4 0.2 collective-permute-start.5
  49.7 0.0 collective-permute-done.4
  49.7 1.8 %collective-permute-start.6 = (bf16[4,1,2,128,256]{4,3,2,0,1:T(8,128)(2,1)S(1)}, bf16[4,1,2,128,256]{4,3,2,0,1:T(8,128)(2,1)S(1)}, u32[]{:S(2)}, u32[]{:S(2)}) collective-permute-start(bf16[4,1,2,128,256]{4,3,2,0,1:T(8,128)(2,1)S(1)} %collective-permute-done.4), channel_id=1, source_target_pairs={{0,4},{8,0},{16,8},{24,16},{28,24},{20,28},{12,20},{4,12},{1,5},{9... | collective-permute-start | bytes 1572872 | tf_op jit(solution)/shard_map/ppermute | solution.py:81
  51.5 0.1 fusion.36
  51.7 0.3 fusion.15
  52.1 9.4 %collective-permute-done.5 = bf16[4,1,2,128,256]{4,3,2,0,1:T(8,128)(2,1)S(1)} collective-permute-done((bf16[4,1,2,128,256]{4,3,2,0,1:T(8,128)(2,1)S(1)}, bf16[4,1,2,128,256]{4,3,2,0,1:T(8,128)(2,1)S(1)}, u32[]{:S(2)}, u32[]{:S(2)}) %collective-permute-start.5) | collective-permute-done | bytes 524320 | tf_op jit(solution)/shard_map/ppermute | solution.py:77
  61.5 0.1 collective-permute-start.7
  61.6 0.3 fusion.14
  62.0 0.2 collective-permute-done.6
  62.2 1.7 %collective-permute-start.8 = (bf16[4,1,2,128,256]{4,3,2,0,1:T(8,128)(2,1)S(1)}, bf16[4,1,2,128,256]{4,3,2,0,1:T(8,128)(2,1)S(1)}, u32[]{:S(2)}, u32[]{:S(2)}) collective-permute-start(bf16[4,1,2,128,256]{4,3,2,0,1:T(8,128)(2,1)S(1)} %collective-permute-done.6), channel_id=1, source_target_pairs={{0,4},{8,0},{16,8},{24,16},{28,24},{20,28},{12,20},{4,12},{1,5},{9... | collective-permute-start | bytes 1572872 | tf_op jit(solution)/shard_map/ppermute | solution.py:81
  64.0 0.3 fusion.13
  64.4 0.3 fusion.12
  64.8 8.0 %collective-permute-done.7 = bf16[4,1,2,128,256]{4,3,2,0,1:T(8,128)(2,1)S(1)} collective-permute-done((bf16[4,1,2,128,256]{4,3,2,0,1:T(8,128)(2,1)S(1)}, bf16[4,1,2,128,256]{4,3,2,0,1:T(8,128)(2,1)S(1)}, u32[]{:S(2)}, u32[]{:S(2)}) %collective-permute-start.7) | collective-permute-done | bytes 524320 | tf_op jit(solution)/shard_map/ppermute | solution.py:77
  72.7 0.4 collective-permute-start.9
  73.1 0.3 fusion.11
  73.5 0.9 collective-permute-done.8
  74.4 0.3 fusion.10
  74.8 0.3 fusion.9
  75.1 9.8 %collective-permute-done.9 = bf16[4,1,2,128,256]{4,3,2,0,1:T(8,128)(2,1)S(1)} collective-permute-done((bf16[4,1,2,128,256]{4,3,2,0,1:T(8,128)(2,1)S(1)}, bf16[4,1,2,128,256]{4,3,2,0,1:T(8,128)(2,1)S(1)}, u32[]{:S(2)}, u32[]{:S(2)}) %collective-permute-start.9) | collective-permute-done | bytes 524320 | tf_op jit(solution)/shard_map/ppermute | solution.py:77
  85.0 0.3 fusion.8
  85.3 0.0 copy-start
  85.3 1.3 %copy-done = f32[8,1,256,256]{3,2,1,0:T(8,128)} copy-done((f32[8,1,256,256]{3,2,1,0:T(8,128)}, f32[8,1,256,256]{3,2,1,0:T(8,128)S(1)}, u32[]{:S(2)}) %copy-start) | copy-done | bytes 2097176
  86.7 2.3 %gather_fusion.1 = f32[8,256,256]{2,1,0:T(8,128)S(1)} fusion(f32[8,256,256]{2,1,0:T(8,128)} %bitcast.123, s32[1024]{0:T(1024)S(1)} %pad_clamp_fusion), kind=kCustom, calls=%fused_computation.1 | custom fusion | bytes 4194336 | tf_op jit(solution)/shard_map/jit(_take)/gather | solution.py:86
  88.9 0.3 fusion.19
  89.3 1.1 %copy.54 = bf16[1,8,2,16,8,256]{5,4,1,3,2,0:T(8,128)(2,1)} copy(bf16[1,8,2,16,8,256]{5,4,3,2,1,0:T(8,128)(2,1)S(1)} %fusion.19) | data formatting | bytes 2097152 | tf_op jit(solution)/shard_map/reshape | solution.py:90
  (22 shorter events, 0.4 us)
Async XLA Ops:
  1.6 8.7 %copy-start.1 = (bf16[1,2,128,2048]{3,2,1,0:T(8,128)(2,1)S(1)}, bf16[1,2,128,2048]{3,2,1,0:T(8,128)(2,1)}, u32[]{:S(2)}) copy-start(bf16[1,2,128,2048]{3,2,1,0:T(8,128)(2,1)} %param.6) | copy-start | bytes 3145732
  1.6 8.7 %copy-start.3 = (s32[4,128]{1,0:T(4,128)S(1)}, s32[4,128]{1,0:T(4,128)}, u32[]{:S(2)}) copy-start(s32[4,128]{1,0:T(4,128)} %param.9) | copy-start | bytes 6148
  3.0 33.1 %all-to-all-start = ((bf16[8,1,2,128,256]{4,3,2,1,0:T(8,128)(2,1)}), bf16[8,1,2,128,256]{4,3,2,1,0:T(8,128)(2,1)S(1)}, u32[]{:S(2)}, u32[]{:S(2)}) async-start(bf16[8,1,2,128,256]{4,3,2,1,0:T(8,128)(2,1)} %copy.44), calls=%async_computation | async-start | bytes 2097152 | tf_op jit(solution)/shard_map/all_to_all | solution.py:57
  10.3 2.6 %copy-start.6 = (s32[8]{0:T(128)S(1)}, s32[8]{0:T(128)}, u32[]{:S(2)}) copy-start(s32[8]{0:T(128)} %constant.108.clone) | copy-start | bytes 100
  10.3 7.1 %copy-start.2 = (s32[8]{0:T(128)S(1)}, s32[8]{0:T(128)}, u32[]{:S(2)}) copy-start(s32[8]{0:T(128)} %constant.107.clone) | copy-start | bytes 100
  10.3 12.9 %copy-start.5 = (s32[4]{0:T(128)S(1)}, s32[4]{0:T(128)}, u32[]{:S(2)}) copy-start(s32[4]{0:T(128)} %param.8) | copy-start | bytes 52
  10.3 12.9 %copy-start.4 = (s32[128,2]{0,1:T(2,128)S(1)}, s32[128,2]{0,1:T(2,128)}, u32[]{:S(2)}) copy-start(s32[128,2]{0,1:T(2,128)} %param.7) | copy-start | bytes 3076
  11.1 27.8 %collective-permute-start.2 = (bf16[1,2,128,512]{2,3,1,0:T(8,128)(2,1)S(1)}, bf16[1,2,128,512]{2,3,1,0:T(8,128)(2,1)S(1)}, u32[]{:S(2)}, u32[]{:S(2)}) collective-permute-start(bf16[1,2,128,512]{2,3,1,0:T(8,128)(2,1)S(1)} %fusion.16), channel_id=1, source_target_pairs={{0,3},{1,0},{2,1},{3,2},{4,7},{5,4},{6,5},{7,6},{8,11},{9,8},{10,9... | collective-permute-start | bytes 786440 | tf_op jit(solution)/shard_map/ppermute | solution.py:29
  11.8 27.1 %collective-permute-start.1 = (bf16[1,2,128,512]{2,3,1,0:T(8,128)(2,1)S(1)}, bf16[1,2,128,512]{2,3,1,0:T(8,128)(2,1)S(1)}, u32[]{:S(2)}, u32[]{:S(2)}) collective-permute-start(bf16[1,2,128,512]{2,3,1,0:T(8,128)(2,1)S(1)} %fusion.16), channel_id=1, source_target_pairs={{0,2},{1,3},{2,0},{3,1},{4,6},{5,7},{6,4},{7,5},{8,10},{9,11},{10,... | collective-permute-start | bytes 786440 | tf_op jit(solution)/shard_map/ppermute | solution.py:29
  12.7 26.1 %collective-permute-start = (bf16[1,2,128,512]{2,3,1,0:T(8,128)(2,1)S(1)}, bf16[1,2,128,512]{2,3,1,0:T(8,128)(2,1)S(1)}, u32[]{:S(2)}, u32[]{:S(2)}) collective-permute-start(bf16[1,2,128,512]{2,3,1,0:T(8,128)(2,1)S(1)} %fusion.16), channel_id=1, source_target_pairs={{0,1},{1,2},{2,3},{3,0},{4,5},{5,6},{6,7},{7,4},{8,9},{9,10},{10,1... | collective-permute-start | bytes 786440 | tf_op jit(solution)/shard_map/ppermute | solution.py:29
  36.7 12.7 %collective-permute-start.3 = (bf16[4,1,2,128,256]{4,3,2,0,1:T(8,128)(2,1)S(1)}, bf16[4,1,2,128,256]{4,3,2,0,1:T(8,128)(2,1)S(1)}, u32[]{:S(2)}, u32[]{:S(2)}) collective-permute-start(bf16[4,1,2,128,256]{4,3,2,0,1:T(8,128)(2,1)S(1)} %bitcast_select_fusion), channel_id=1, source_target_pairs={{0,8},{8,16},{16,24},{24,28},{28,20},{20,12},{12,4},{4,0},{1,9},{9... | collective-permute-start | bytes 1572872 | tf_op jit(solution)/shard_map/ppermute | solution.py:77
  36.8 12.8 %collective-permute-start.4 = (bf16[4,1,2,128,256]{4,3,2,0,1:T(8,128)(2,1)S(1)}, bf16[4,1,2,128,256]{4,3,2,0,1:T(8,128)(2,1)S(1)}, u32[]{:S(2)}, u32[]{:S(2)}) collective-permute-start(bf16[4,1,2,128,256]{4,3,2,0,1:T(8,128)(2,1)S(1)} %bitcast_select_fusion), channel_id=1, source_target_pairs={{0,4},{8,0},{16,8},{24,16},{28,24},{20,28},{12,20},{4,12},{1,5},{9... | collective-permute-start | bytes 1572872 | tf_op jit(solution)/shard_map/ppermute | solution.py:81
  49.4 12.1 %collective-permute-start.5 = (bf16[4,1,2,128,256]{4,3,2,0,1:T(8,128)(2,1)S(1)}, bf16[4,1,2,128,256]{4,3,2,0,1:T(8,128)(2,1)S(1)}, u32[]{:S(2)}, u32[]{:S(2)}) collective-permute-start(bf16[4,1,2,128,256]{4,3,2,0,1:T(8,128)(2,1)S(1)} %collective-permute-done.3), channel_id=1, source_target_pairs={{0,8},{8,16},{16,24},{24,28},{28,20},{20,12},{12,4},{4,0},{1,9},{9... | collective-permute-start | bytes 1572872 | tf_op jit(solution)/shard_map/ppermute | solution.py:77
  49.7 12.6 %collective-permute-start.6 = (bf16[4,1,2,128,256]{4,3,2,0,1:T(8,128)(2,1)S(1)}, bf16[4,1,2,128,256]{4,3,2,0,1:T(8,128)(2,1)S(1)}, u32[]{:S(2)}, u32[]{:S(2)}) collective-permute-start(bf16[4,1,2,128,256]{4,3,2,0,1:T(8,128)(2,1)S(1)} %collective-permute-done.4), channel_id=1, source_target_pairs={{0,4},{8,0},{16,8},{24,16},{28,24},{20,28},{12,20},{4,12},{1,5},{9... | collective-permute-start | bytes 1572872 | tf_op jit(solution)/shard_map/ppermute | solution.py:81
  61.5 11.2 %collective-permute-start.7 = (bf16[4,1,2,128,256]{4,3,2,0,1:T(8,128)(2,1)S(1)}, bf16[4,1,2,128,256]{4,3,2,0,1:T(8,128)(2,1)S(1)}, u32[]{:S(2)}, u32[]{:S(2)}) collective-permute-start(bf16[4,1,2,128,256]{4,3,2,0,1:T(8,128)(2,1)S(1)} %collective-permute-done.5), channel_id=1, source_target_pairs={{0,8},{8,16},{16,24},{24,28},{28,20},{20,12},{12,4},{4,0},{1,9},{9... | collective-permute-start | bytes 1572872 | tf_op jit(solution)/shard_map/ppermute | solution.py:77
  62.2 12.2 %collective-permute-start.8 = (bf16[4,1,2,128,256]{4,3,2,0,1:T(8,128)(2,1)S(1)}, bf16[4,1,2,128,256]{4,3,2,0,1:T(8,128)(2,1)S(1)}, u32[]{:S(2)}, u32[]{:S(2)}) collective-permute-start(bf16[4,1,2,128,256]{4,3,2,0,1:T(8,128)(2,1)S(1)} %collective-permute-done.6), channel_id=1, source_target_pairs={{0,4},{8,0},{16,8},{24,16},{28,24},{20,28},{12,20},{4,12},{1,5},{9... | collective-permute-start | bytes 1572872 | tf_op jit(solution)/shard_map/ppermute | solution.py:81
  72.7 12.2 %collective-permute-start.9 = (bf16[4,1,2,128,256]{4,3,2,0,1:T(8,128)(2,1)S(1)}, bf16[4,1,2,128,256]{4,3,2,0,1:T(8,128)(2,1)S(1)}, u32[]{:S(2)}, u32[]{:S(2)}) collective-permute-start(bf16[4,1,2,128,256]{4,3,2,0,1:T(8,128)(2,1)S(1)} %collective-permute-done.7), channel_id=1, source_target_pairs={{0,8},{8,16},{16,24},{24,28},{28,20},{20,12},{12,4},{4,0},{1,9},{9... | collective-permute-start | bytes 1572872 | tf_op jit(solution)/shard_map/ppermute | solution.py:77
  85.3 1.3 %copy-start = (f32[8,1,256,256]{3,2,1,0:T(8,128)}, f32[8,1,256,256]{3,2,1,0:T(8,128)S(1)}, u32[]{:S(2)}) copy-start(f32[8,1,256,256]{3,2,1,0:T(8,128)S(1)} %fusion.8) | copy-start | bytes 6291460

commit v2 on v1

--- a/solution.py
+++ b/solution.py
@@ -53,8 +53,8 @@
         [jnp.concatenate([nr, -ni], axis=2), jnp.concatenate([ni, nr], axis=2)], axis=1
     )
 
-    pieces = records.reshape(freqs, parts, shots_here, n_shot, width).transpose(3, 0, 1, 2, 4)
-    pieces = lax.all_to_all(pieces, "shot", 0, 0, tiled=True)
+    pieces = lax.all_to_all(records, "shot", 3, 0, tiled=True)
+    pieces = pieces.reshape(n_shot, freqs, parts, shots_here, width)
     mine = jnp.take(pieces, block_owner, axis=0)
 
     order = ring_order(n_shot)
@@ -68,25 +68,30 @@
     backward = [(order[k], order[(k - 1) % n_shot]) for k in range(n_shot)]
     n_fwd = n_shot // 2
     n_bwd = n_shot - 1 - n_fwd
+    split_last = n_fwd > n_bwd and width % 2 == 0
+    half = width // 2
 
-    outs = [piece_product(lhs, mine)]
-    came_from = [me]
+    factor = (2.0 * APER * BLOCK) ** (-0.5)
+    total = jnp.zeros((freqs, parts * shots_here, rcv_here), jnp.bfloat16)
+
+    def place(total, piece, source):
+        product = (piece_product(lhs, piece) * factor).astype(jnp.bfloat16)
+        return lax.dynamic_update_slice_in_dim(total, product, source * width, axis=2)
+
+    total = place(total, mine, me)
     fwd, bwd = mine, mine
     for t in range(1, max(n_fwd, n_bwd) + 1):
+        if t == n_fwd and split_last:
+            first = lax.ppermute(fwd[..., :half], "shot", forward)
+            second = lax.ppermute(bwd[..., half:], "shot", backward)
+            total = place(total, jnp.concatenate([first, second], axis=-1), order_arr[(pos - t) % n_shot])
+            continue
         if t <= n_fwd:
             fwd = lax.ppermute(fwd, "shot", forward)
-            outs.append(piece_product(lhs, fwd))
-            came_from.append(order_arr[(pos - t) % n_shot])
+            total = place(total, fwd, order_arr[(pos - t) % n_shot])
         if t <= n_bwd:
             bwd = lax.ppermute(bwd, "shot", backward)
-            outs.append(piece_product(lhs, bwd))
-            came_from.append(order_arr[(pos + t) % n_shot])
-    came_from = jnp.stack(came_from)
-    arrival = jnp.zeros((n_shot,), jnp.int32).at[came_from].set(jnp.arange(n_shot, dtype=jnp.int32))
-    stacked = jnp.take(jnp.stack(outs), arrival, axis=0)
-    factor = (2.0 * APER * BLOCK) ** (-0.5)
-    total = (stacked * factor).astype(jnp.bfloat16)
-    total = total.reshape(n_shot, freqs, parts, shots_here, width).transpose(1, 2, 3, 0, 4)
+            total = place(total, bwd, order_arr[(pos + t) % n_shot])
     return total.reshape(freqs, parts, shots_here, rcv_here)
 
 

time: 90.7 us -> 85.4 us (0.942)
  local copies, waits for them, and re-layouts: 14.8 us -> 7.84 us
  waiting for transfers between devices: 51.3 us -> 45 us
  between operations: 4.34 us -> 9.82 us
  starting transfers between devices: 15.5 us -> 18.2 us
    ppermute x4 -> x3, waiting for transfers between devices: 37.5 us -> 27.3 us  [per_device(): fwd = lax.ppermute(fwd, 'shot', forward)]
    ppermute x0 -> x2, waiting for transfers between devices: none -> 4.71 us  [the longest x1 3.48 us: per_device(): second = lax.ppermute(bwd[..., half:], 'shot', backward)]
    another operation x1 -> x0, local copies, waits for them, and re-layouts: 4.45 us -> none  [per_device(): came_from = jnp.stack(came_from)]
    gather x1 -> x0, local copies, waits for them, and re-layouts: 2.27 us -> none  [per_device(): stacked = jnp.take(jnp.stack(outs), arrival, axis=0)]
    ppermute x0 -> x2, starting transfers between devices: none -> 2.13 us  [the longest x1 1.18 us: per_device(): second = lax.ppermute(bwd[..., half:], 'shot', backward)]
    all_to_all x1, waiting for transfers between devices: 12.8 us -> 10.9 us  [per_device(): pieces = lax.all_to_all(records, 'shot', 3, 0, tiled=True)]
    unnamed x15, local copies, waits for them, and re-layouts: 2.97 us -> 4.66 us
    transpose x1 -> x0, local copies, waits for them, and re-layouts: 1.31 us -> none  [per_device(): records.reshape(freqs, parts, shots_here, n_shot, width)]
  transfers between devices with their start and end apart: 11 -> 12, of which waited for: 7 -> 8; matrix products, arithmetic and copies ran while one was open for 12% -> 8% of each run, Pallas kernels for 0% -> 0%
where the time goes in v2:
time: 85.4 us; the launch traced here: 85 us
  waiting for transfers between devices  45 us (53%)
  starting transfers between devices  18.2 us (21%)
  between operations  9.82 us (11%)
  local copies, waits for them, and re-layouts  7.84 us (9%)
  matrix products  3.62 us (4%)
    ppermute x3, waiting for transfers between devices, per_device(): fwd = lax.ppermute(fwd, 'shot', forward)  27.3 us
    all_to_all x1, waiting for transfers between devices, per_device(): pieces = lax.all_to_all(records, 'shot', 3, 0, tiled=True)  10.9 us
    all_to_all x1, starting transfers between devices, per_device(): pieces = lax.all_to_all(records, 'shot', 3, 0, tiled=True)  7.44 us
    ppermute x3, starting transfers between devices, per_device(): bwd = lax.ppermute(bwd, 'shot', backward)  5.16 us
    unnamed x15, local copies, waits for them, and re-layouts  4.66 us
    ppermute x1, waiting for transfers between devices, per_device(): second = lax.ppermute(bwd[..., half:], 'shot', backward)  3.48 us
    ppermute x3, starting transfers between devices, gather_near(): lax.ppermute(picked, 'rcv', [(i, (i + k) % n_rcv) for i in range(n_rcv)])  2.99 us
    dot_general x8, matrix products, piece_product(): jnp.einsum('fsk,fkw->fsw', lhs, rhs, preferred_element_type=jnp.float32)  2.84 us
  transfers between devices with their start and end apart: 12, of which 8 were waited for; matrix products, arithmetic and copies ran while one was open for 8% of the time, Pallas kernels for 0%

profile of v2, /device:TPU:0, one launch (start us, length us, event | category | flops | bytes accessed | tf_op | source)
XLA Modules:
  0.0 85.0 jit_solution(15699327598307794268)
XLA Ops:
  0.0 3.7 %copy.40 = bf16[1,2,128,2048]{2,1,0,3:T(2,128)(2,1)} copy(bf16[1,2,128,2048]{3,2,1,0:T(8,128)(2,1)} %param.6) | data formatting | bytes 2097152 | tf_op args[0]
  3.7 0.0 copy-start
  3.7 0.0 copy-start.3
  3.7 7.4 %all-to-all-start = ((bf16[1,2,128,2048]{2,1,0,3:T(2,128)(2,1)}), bf16[1,2,128,2048]{2,1,0,3:T(2,128)(2,1)S(1)}, u32[]{:S(2)}, u32[]{:S(2)}) async-start(bf16[1,2,128,2048]{2,1,0,3:T(2,128)(2,1)} %copy.40), calls=%async_computation | async-start | bytes 2097152 | tf_op jit(solution)/shard_map/all_to_all | solution.py:56
  11.1 0.0 copy-done
  11.1 0.0 copy-done.3
  11.1 0.0 copy-start.4
  11.1 0.0 copy-start.5
  11.2 0.0 copy-start.6
  11.2 0.0 copy-start.2
  11.2 0.8 fusion.8
  12.0 0.1 collective-permute-start
  12.0 1.5 %collective-permute-start.1 = (bf16[1,2,128,512]{2,3,1,0:T(8,128)(2,1)S(1)}, bf16[1,2,128,512]{2,3,1,0:T(8,128)(2,1)S(1)}, u32[]{:S(2)}, u32[]{:S(2)}) collective-permute-start(bf16[1,2,128,512]{2,3,1,0:T(8,128)(2,1)S(1)} %fusion.8), channel_id=1, source_target_pairs={{0,2},{1,3},{2,0},{3,1},{4,6},{5,7},{6,4},{7,5},{8,10},{9,11},{10,... | collective-permute-start | bytes 786440 | tf_op jit(solution)/shard_map/ppermute | solution.py:29
  13.6 1.4 %collective-permute-start.2 = (bf16[1,2,128,512]{2,3,1,0:T(8,128)(2,1)S(1)}, bf16[1,2,128,512]{2,3,1,0:T(8,128)(2,1)S(1)}, u32[]{:S(2)}, u32[]{:S(2)}) collective-permute-start(bf16[1,2,128,512]{2,3,1,0:T(8,128)(2,1)S(1)} %fusion.8), channel_id=1, source_target_pairs={{0,3},{1,0},{2,1},{3,2},{4,7},{5,4},{6,5},{7,6},{8,11},{9,8},{10,9... | collective-permute-start | bytes 786440 | tf_op jit(solution)/shard_map/ppermute | solution.py:29
  15.0 0.0 copy-done.4
  15.0 0.0 copy-done.5
  15.0 0.0 copy-done.6
  15.1 0.7 dynamic_slice.24
  20.7 0.0 copy-done.2
  20.7 0.7 fusion.39
  25.9 10.9 %all-to-all-done = bf16[1,2,128,2048]{2,1,0,3:T(2,128)(2,1)S(1)} async-done(((bf16[1,2,128,2048]{2,1,0,3:T(2,128)(2,1)}), bf16[1,2,128,2048]{2,1,0,3:T(2,128)(2,1)S(1)}, u32[]{:S(2)}, u32[]{:S(2)}) %all-to-all-start) | async-done | bytes 1048608 | tf_op jit(solution)/shard_map/all_to_all | solution.py:56
  36.9 0.7 copy.42
  37.6 0.6 gather_fusion
  38.2 0.1 bitcast_select_fusion
  38.3 0.1 collective-permute-start.3
  38.4 2.0 %collective-permute-start.4 = (bf16[4,1,2,128,256]{4,3,2,0,1:T(8,128)(2,1)S(1)}, bf16[4,1,2,128,256]{4,3,2,0,1:T(8,128)(2,1)S(1)}, u32[]{:S(2)}, u32[]{:S(2)}) collective-permute-start(bf16[4,1,2,128,256]{4,3,2,0,1:T(8,128)(2,1)S(1)} %bitcast_select_fusion), channel_id=1, source_target_pairs={{0,4},{8,0},{16,8},{24,16},{28,24},{20,28},{12,20},{4,12},{1,5},{9... | collective-permute-start | bytes 1572872 | tf_op jit(solution)/shard_map/ppermute | solution.py:93
  40.4 0.0 collective-permute-done
  40.4 0.0 collective-permute-done.1
  40.4 0.0 collective-permute-done.2
  40.4 0.2 fusion.36
  40.6 10.3 %collective-permute-done.3 = bf16[4,1,2,128,256]{4,3,2,0,1:T(8,128)(2,1)S(1)} collective-permute-done((bf16[4,1,2,128,256]{4,3,2,0,1:T(8,128)(2,1)S(1)}, bf16[4,1,2,128,256]{4,3,2,0,1:T(8,128)(2,1)S(1)}, u32[]{:S(2)}, u32[]{:S(2)}) %collective-permute-start.3) | collective-permute-done | bytes 524320 | tf_op jit(solution)/shard_map/ppermute | solution.py:90
  51.0 0.2 collective-permute-start.5
  51.2 0.0 collective-permute-done.4
  51.2 1.8 %collective-permute-start.6 = (bf16[4,1,2,128,256]{4,3,2,0,1:T(8,128)(2,1)S(1)}, bf16[4,1,2,128,256]{4,3,2,0,1:T(8,128)(2,1)S(1)}, u32[]{:S(2)}, u32[]{:S(2)}) collective-permute-start(bf16[4,1,2,128,256]{4,3,2,0,1:T(8,128)(2,1)S(1)} %collective-permute-done.4), channel_id=1, source_target_pairs={{0,4},{8,0},{16,8},{24,16},{28,24},{20,28},{12,20},{4,12},{1,5},{9... | collective-permute-start | bytes 1572872 | tf_op jit(solution)/shard_map/ppermute | solution.py:93
  53.0 0.1 fusion.48
  53.2 0.1 broadcast_in_dim.17
  53.3 0.4 fusion.34
  53.7 0.4 fusion.32
  54.1 9.0 %collective-permute-done.5 = bf16[4,1,2,128,256]{4,3,2,0,1:T(8,128)(2,1)S(1)} collective-permute-done((bf16[4,1,2,128,256]{4,3,2,0,1:T(8,128)(2,1)S(1)}, bf16[4,1,2,128,256]{4,3,2,0,1:T(8,128)(2,1)S(1)}, u32[]{:S(2)}, u32[]{:S(2)}) %collective-permute-start.5) | collective-permute-done | bytes 524320 | tf_op jit(solution)/shard_map/ppermute | solution.py:90
  63.1 0.1 collective-permute-start.7
  63.2 0.5 collective-permute-done.6
  63.7 1.4 %collective-permute-start.8 = (bf16[4,1,2,128,256]{4,3,2,0,1:T(8,128)(2,1)S(1)}, bf16[4,1,2,128,256]{4,3,2,0,1:T(8,128)(2,1)S(1)}, u32[]{:S(2)}, u32[]{:S(2)}) collective-permute-start(bf16[4,1,2,128,256]{4,3,2,0,1:T(8,128)(2,1)S(1)} %collective-permute-done.6), channel_id=1, source_target_pairs={{0,4},{8,0},{16,8},{24,16},{28,24},{20,28},{12,20},{4,12},{1,5},{9... | collective-permute-start | bytes 1572872 | tf_op jit(solution)/shard_map/ppermute | solution.py:93
  65.1 0.4 fusion.30
  65.5 0.4 fusion.28
  65.9 0.4 fusion.26
  66.3 8.0 %collective-permute-done.7 = bf16[4,1,2,128,256]{4,3,2,0,1:T(8,128)(2,1)S(1)} collective-permute-done((bf16[4,1,2,128,256]{4,3,2,0,1:T(8,128)(2,1)S(1)}, bf16[4,1,2,128,256]{4,3,2,0,1:T(8,128)(2,1)S(1)}, u32[]{:S(2)}, u32[]{:S(2)}) %collective-permute-start.7) | collective-permute-done | bytes 524320 | tf_op jit(solution)/shard_map/ppermute | solution.py:90
  74.3 1.5 %collective-permute-done.8 = bf16[4,1,2,128,256]{4,3,2,0,1:T(8,128)(2,1)S(1)} collective-permute-done((bf16[4,1,2,128,256]{4,3,2,0,1:T(8,128)(2,1)S(1)}, bf16[4,1,2,128,256]{4,3,2,0,1:T(8,128)(2,1)S(1)}, u32[]{:S(2)}, u32[]{:S(2)}) %collective-permute-start.8) | collective-permute-done | bytes 524320 | tf_op jit(solution)/shard_map/ppermute | solution.py:93
  75.9 1.2 %collective-permute-start.10 = (bf16[4,1,2,128,128]{4,3,2,0,1:T(8,128)(2,1)S(1)}, bf16[4,1,2,128,128]{4,3,2,0,1:T(8,128)(2,1)S(1)}, u32[]{:S(2)}, u32[]{:S(2)}) collective-permute-start(bf16[4,1,2,128,128]{4,3,2,0,1:T(8,128)(2,1)S(1)} %slice.21), channel_id=1, source_target_pairs={{0,4},{8,0},{16,8},{24,16},{28,24},{20,28},{12,20},{4,12},{1,5},{9... | collective-permute-start | bytes 786440 | tf_op jit(solution)/shard_map/ppermute | solution.py:86
  77.1 0.9 %collective-permute-start.9 = (bf16[4,1,2,128,128]{4,3,2,0,1:T(8,128)(2,1)S(1)}, bf16[4,1,2,128,128]{4,3,2,0,1:T(8,128)(2,1)S(1)}, u32[]{:S(2)}, u32[]{:S(2)}) collective-permute-start(bf16[4,1,2,128,128]{4,3,2,0,1:T(8,128)(2,1)S(1)} %slice.20), channel_id=1, source_target_pairs={{0,8},{8,16},{16,24},{24,28},{28,20},{20,12},{12,4},{4,0},{1,9},{9... | collective-permute-start | bytes 786440 | tf_op jit(solution)/shard_map/ppermute | solution.py:85
  78.1 0.4 fusion.24
  78.5 0.4 fusion.22
  78.9 3.5 %collective-permute-done.10 = bf16[4,1,2,128,128]{4,3,2,0,1:T(8,128)(2,1)S(1)} collective-permute-done((bf16[4,1,2,128,128]{4,3,2,0,1:T(8,128)(2,1)S(1)}, bf16[4,1,2,128,128]{4,3,2,0,1:T(8,128)(2,1)S(1)}, u32[]{:S(2)}, u32[]{:S(2)}) %collective-permute-start.10) | collective-permute-done | bytes 262176 | tf_op jit(solution)/shard_map/ppermute | solution.py:86
  82.3 1.2 %collective-permute-done.9 = bf16[4,1,2,128,128]{4,3,2,0,1:T(8,128)(2,1)S(1)} collective-permute-done((bf16[4,1,2,128,128]{4,3,2,0,1:T(8,128)(2,1)S(1)}, bf16[4,1,2,128,128]{4,3,2,0,1:T(8,128)(2,1)S(1)}, u32[]{:S(2)}, u32[]{:S(2)}) %collective-permute-start.9) | collective-permute-done | bytes 262176 | tf_op jit(solution)/shard_map/ppermute | solution.py:85
  83.6 0.1 maximum_bitcast_fusion.1
  83.7 0.4 fusion.20
  84.0 0.0 copy-start.1
  84.1 1.0 %copy-done.1 = bf16[1,256,2048]{2,1,0:T(8,128)(2,1)} copy-done((bf16[1,256,2048]{2,1,0:T(8,128)(2,1)}, bf16[1,256,2048]{2,1,0:T(8,128)(2,1)S(1)}, u32[]{:S(2)}) %copy-start.1) | copy-done | bytes 1048600
  (19 shorter events, 0.5 us)
Async XLA Ops:
  3.7 7.5 %copy-start = (bf16[1,2,128,2048]{3,2,1,0:T(8,128)(2,1)S(1)}, bf16[1,2,128,2048]{3,2,1,0:T(8,128)(2,1)}, u32[]{:S(2)}) copy-start(bf16[1,2,128,2048]{3,2,1,0:T(8,128)(2,1)} %param.6) | copy-start | bytes 3145732
  3.7 7.5 %copy-start.3 = (s32[4,128]{1,0:T(4,128)S(1)}, s32[4,128]{1,0:T(4,128)}, u32[]{:S(2)}) copy-start(s32[4,128]{1,0:T(4,128)} %param.9) | copy-start | bytes 6148
  3.7 33.2 %all-to-all-start = ((bf16[1,2,128,2048]{2,1,0,3:T(2,128)(2,1)}), bf16[1,2,128,2048]{2,1,0,3:T(2,128)(2,1)S(1)}, u32[]{:S(2)}, u32[]{:S(2)}) async-start(bf16[1,2,128,2048]{2,1,0,3:T(2,128)(2,1)} %copy.40), calls=%async_computation | async-start | bytes 2097152 | tf_op jit(solution)/shard_map/all_to_all | solution.py:56
  11.1 3.8 %copy-start.4 = (s32[128,2]{0,1:T(2,128)S(1)}, s32[128,2]{0,1:T(2,128)}, u32[]{:S(2)}) copy-start(s32[128,2]{0,1:T(2,128)} %param.7) | copy-start | bytes 3076
  11.1 3.8 %copy-start.5 = (s32[4]{0:T(128)S(1)}, s32[4]{0:T(128)}, u32[]{:S(2)}) copy-start(s32[4]{0:T(128)} %param.8) | copy-start | bytes 52
  11.2 3.9 %copy-start.6 = (s32[8]{0:T(128)S(1)}, s32[8]{0:T(128)}, u32[]{:S(2)}) copy-start(s32[8]{0:T(128)} %constant.105.clone) | copy-start | bytes 100
  11.2 9.5 %copy-start.2 = (s32[8]{0:T(128)S(1)}, s32[8]{0:T(128)}, u32[]{:S(2)}) copy-start(s32[8]{0:T(128)} %constant.104.clone) | copy-start | bytes 100
  12.0 28.4 %collective-permute-start = (bf16[1,2,128,512]{2,3,1,0:T(8,128)(2,1)S(1)}, bf16[1,2,128,512]{2,3,1,0:T(8,128)(2,1)S(1)}, u32[]{:S(2)}, u32[]{:S(2)}) collective-permute-start(bf16[1,2,128,512]{2,3,1,0:T(8,128)(2,1)S(1)} %fusion.8), channel_id=1, source_target_pairs={{0,1},{1,2},{2,3},{3,0},{4,5},{5,6},{6,7},{7,4},{8,9},{9,10},{10,1... | collective-permute-start | bytes 786440 | tf_op jit(solution)/shard_map/ppermute | solution.py:29
  12.0 28.3 %collective-permute-start.1 = (bf16[1,2,128,512]{2,3,1,0:T(8,128)(2,1)S(1)}, bf16[1,2,128,512]{2,3,1,0:T(8,128)(2,1)S(1)}, u32[]{:S(2)}, u32[]{:S(2)}) collective-permute-start(bf16[1,2,128,512]{2,3,1,0:T(8,128)(2,1)S(1)} %fusion.8), channel_id=1, source_target_pairs={{0,2},{1,3},{2,0},{3,1},{4,6},{5,7},{6,4},{7,5},{8,10},{9,11},{10,... | collective-permute-start | bytes 786440 | tf_op jit(solution)/shard_map/ppermute | solution.py:29
  13.6 26.8 %collective-permute-start.2 = (bf16[1,2,128,512]{2,3,1,0:T(8,128)(2,1)S(1)}, bf16[1,2,128,512]{2,3,1,0:T(8,128)(2,1)S(1)}, u32[]{:S(2)}, u32[]{:S(2)}) collective-permute-start(bf16[1,2,128,512]{2,3,1,0:T(8,128)(2,1)S(1)} %fusion.8), channel_id=1, source_target_pairs={{0,3},{1,0},{2,1},{3,2},{4,7},{5,4},{6,5},{7,6},{8,11},{9,8},{10,9... | collective-permute-start | bytes 786440 | tf_op jit(solution)/shard_map/ppermute | solution.py:29
  38.3 12.7 %collective-permute-start.3 = (bf16[4,1,2,128,256]{4,3,2,0,1:T(8,128)(2,1)S(1)}, bf16[4,1,2,128,256]{4,3,2,0,1:T(8,128)(2,1)S(1)}, u32[]{:S(2)}, u32[]{:S(2)}) collective-permute-start(bf16[4,1,2,128,256]{4,3,2,0,1:T(8,128)(2,1)S(1)} %bitcast_select_fusion), channel_id=1, source_target_pairs={{0,8},{8,16},{16,24},{24,28},{28,20},{20,12},{12,4},{4,0},{1,9},{9... | collective-permute-start | bytes 1572872 | tf_op jit(solution)/shard_map/ppermute | solution.py:90
  38.4 12.8 %collective-permute-start.4 = (bf16[4,1,2,128,256]{4,3,2,0,1:T(8,128)(2,1)S(1)}, bf16[4,1,2,128,256]{4,3,2,0,1:T(8,128)(2,1)S(1)}, u32[]{:S(2)}, u32[]{:S(2)}) collective-permute-start(bf16[4,1,2,128,256]{4,3,2,0,1:T(8,128)(2,1)S(1)} %bitcast_select_fusion), channel_id=1, source_target_pairs={{0,4},{8,0},{16,8},{24,16},{28,24},{20,28},{12,20},{4,12},{1,5},{9... | collective-permute-start | bytes 1572872 | tf_op jit(solution)/shard_map/ppermute | solution.py:93
  51.0 12.1 %collective-permute-start.5 = (bf16[4,1,2,128,256]{4,3,2,0,1:T(8,128)(2,1)S(1)}, bf16[4,1,2,128,256]{4,3,2,0,1:T(8,128)(2,1)S(1)}, u32[]{:S(2)}, u32[]{:S(2)}) collective-permute-start(bf16[4,1,2,128,256]{4,3,2,0,1:T(8,128)(2,1)S(1)} %collective-permute-done.3), channel_id=1, source_target_pairs={{0,8},{8,16},{16,24},{24,28},{28,20},{20,12},{12,4},{4,0},{1,9},{9... | collective-permute-start | bytes 1572872 | tf_op jit(solution)/shard_map/ppermute | solution.py:90
  51.2 12.5 %collective-permute-start.6 = (bf16[4,1,2,128,256]{4,3,2,0,1:T(8,128)(2,1)S(1)}, bf16[4,1,2,128,256]{4,3,2,0,1:T(8,128)(2,1)S(1)}, u32[]{:S(2)}, u32[]{:S(2)}) collective-permute-start(bf16[4,1,2,128,256]{4,3,2,0,1:T(8,128)(2,1)S(1)} %collective-permute-done.4), channel_id=1, source_target_pairs={{0,4},{8,0},{16,8},{24,16},{28,24},{20,28},{12,20},{4,12},{1,5},{9... | collective-permute-start | bytes 1572872 | tf_op jit(solution)/shard_map/ppermute | solution.py:93
  63.1 11.2 %collective-permute-start.7 = (bf16[4,1,2,128,256]{4,3,2,0,1:T(8,128)(2,1)S(1)}, bf16[4,1,2,128,256]{4,3,2,0,1:T(8,128)(2,1)S(1)}, u32[]{:S(2)}, u32[]{:S(2)}) collective-permute-start(bf16[4,1,2,128,256]{4,3,2,0,1:T(8,128)(2,1)S(1)} %collective-permute-done.5), channel_id=1, source_target_pairs={{0,8},{8,16},{16,24},{24,28},{28,20},{20,12},{12,4},{4,0},{1,9},{9... | collective-permute-start | bytes 1572872 | tf_op jit(solution)/shard_map/ppermute | solution.py:90
  63.7 12.1 %collective-permute-start.8 = (bf16[4,1,2,128,256]{4,3,2,0,1:T(8,128)(2,1)S(1)}, bf16[4,1,2,128,256]{4,3,2,0,1:T(8,128)(2,1)S(1)}, u32[]{:S(2)}, u32[]{:S(2)}) collective-permute-start(bf16[4,1,2,128,256]{4,3,2,0,1:T(8,128)(2,1)S(1)} %collective-permute-done.6), channel_id=1, source_target_pairs={{0,4},{8,0},{16,8},{24,16},{28,24},{20,28},{12,20},{4,12},{1,5},{9... | collective-permute-start | bytes 1572872 | tf_op jit(solution)/shard_map/ppermute | solution.py:93
  75.9 6.4 %collective-permute-start.10 = (bf16[4,1,2,128,128]{4,3,2,0,1:T(8,128)(2,1)S(1)}, bf16[4,1,2,128,128]{4,3,2,0,1:T(8,128)(2,1)S(1)}, u32[]{:S(2)}, u32[]{:S(2)}) collective-permute-start(bf16[4,1,2,128,128]{4,3,2,0,1:T(8,128)(2,1)S(1)} %slice.21), channel_id=1, source_target_pairs={{0,4},{8,0},{16,8},{24,16},{28,24},{20,28},{12,20},{4,12},{1,5},{9... | collective-permute-start | bytes 786440 | tf_op jit(solution)/shard_map/ppermute | solution.py:86
  77.1 6.4 %collective-permute-start.9 = (bf16[4,1,2,128,128]{4,3,2,0,1:T(8,128)(2,1)S(1)}, bf16[4,1,2,128,128]{4,3,2,0,1:T(8,128)(2,1)S(1)}, u32[]{:S(2)}, u32[]{:S(2)}) collective-permute-start(bf16[4,1,2,128,128]{4,3,2,0,1:T(8,128)(2,1)S(1)} %slice.20), channel_id=1, source_target_pairs={{0,8},{8,16},{16,24},{24,28},{28,20},{20,12},{12,4},{4,0},{1,9},{9... | collective-permute-start | bytes 786440 | tf_op jit(solution)/shard_map/ppermute | solution.py:85
  84.0 1.0 %copy-start.1 = (bf16[1,256,2048]{2,1,0:T(8,128)(2,1)}, bf16[1,256,2048]{2,1,0:T(8,128)(2,1)S(1)}, u32[]{:S(2)}) copy-start(bf16[1,256,2048]{2,1,0:T(8,128)(2,1)S(1)} %fusion.20) | copy-start | bytes 3145732

commit v3 on v2

--- a/solution.py
+++ b/solution.py
@@ -40,7 +40,6 @@
 def per_device(records, aperture, block_owner, block_receivers, n_shot, n_rcv):
     freqs, parts, shots_here, rcv_here = records.shape
     nblocks, block_extent = block_receivers.shape
-    width = rcv_here // n_shot
 
     picked = local_columns(records, block_receivers)
     near = gather_near(picked, n_rcv)
@@ -53,10 +52,6 @@
         [jnp.concatenate([nr, -ni], axis=2), jnp.concatenate([ni, nr], axis=2)], axis=1
     )
 
-    pieces = lax.all_to_all(records, "shot", 3, 0, tiled=True)
-    pieces = pieces.reshape(n_shot, freqs, parts, shots_here, width)
-    mine = jnp.take(pieces, block_owner, axis=0)
-
     order = ring_order(n_shot)
     where = [0] * n_shot
     for k, d in enumerate(order):
@@ -68,30 +63,40 @@
     backward = [(order[k], order[(k - 1) % n_shot]) for k in range(n_shot)]
     n_fwd = n_shot // 2
     n_bwd = n_shot - 1 - n_fwd
-    split_last = n_fwd > n_bwd and width % 2 == 0
-    half = width // 2
 
-    factor = (2.0 * APER * BLOCK) ** (-0.5)
-    total = jnp.zeros((freqs, parts * shots_here, rcv_here), jnp.bfloat16)
+    rows = shots_here // n_shot
+    split_last = n_fwd > n_bwd and rcv_here % 2 == 0
+    half = rcv_here // 2
+    nk = lhs.shape[2]
+    lhs_rows = lhs.reshape(freqs, 2 * shots_here, nk // block_extent, block_extent)
 
-    def place(total, piece, source):
-        product = (piece_product(lhs, piece) * factor).astype(jnp.bfloat16)
-        return lax.dynamic_update_slice_in_dim(total, product, source * width, axis=2)
+    def add(total, piece, source):
+        part = lax.dynamic_slice_in_dim(lhs_rows, source * rows, rows, axis=3)
+        part = part.reshape(freqs, 2 * shots_here, -1)
+        rhs = piece.transpose(1, 2, 0, 3, 4).reshape(freqs, -1, rcv_here)
+        return total + jnp.einsum("fsk,fkw->fsw", part, rhs, preferred_element_type=jnp.float32)
 
-    total = place(total, mine, me)
+    pieces = lax.all_to_all(records, "shot", 2, 0, tiled=True)
+    pieces = pieces.reshape(n_shot, freqs, parts, rows, rcv_here)
+    mine = jnp.take(pieces, block_owner, axis=0)
+
+    total = add(jnp.zeros((freqs, 2 * shots_here, rcv_here), jnp.float32), mine, me)
     fwd, bwd = mine, mine
     for t in range(1, max(n_fwd, n_bwd) + 1):
         if t == n_fwd and split_last:
             first = lax.ppermute(fwd[..., :half], "shot", forward)
             second = lax.ppermute(bwd[..., half:], "shot", backward)
-            total = place(total, jnp.concatenate([first, second], axis=-1), order_arr[(pos - t) % n_shot])
+            joined = jnp.concatenate([first, second], axis=-1)
+            total = add(total, joined, order_arr[(pos - t) % n_shot])
             continue
         if t <= n_fwd:
             fwd = lax.ppermute(fwd, "shot", forward)
-            total = place(total, fwd, order_arr[(pos - t) % n_shot])
+            total = add(total, fwd, order_arr[(pos - t) % n_shot])
         if t <= n_bwd:
             bwd = lax.ppermute(bwd, "shot", backward)
-            total = place(total, bwd, order_arr[(pos + t) % n_shot])
+            total = add(total, bwd, order_arr[(pos + t) % n_shot])
+    factor = (2.0 * APER * BLOCK) ** (-0.5)
+    total = (total * factor).astype(jnp.bfloat16)
     return total.reshape(freqs, parts, shots_here, rcv_here)
 
 

time: 85.4 us -> 84.4 us (0.988)
  matrix products: 3.62 us -> 5.47 us
  local copies, waits for them, and re-layouts: 7.84 us -> 6.15 us
  waiting for transfers between devices: 45 us -> 43.4 us
    ppermute x3, waiting for transfers between devices: 27.3 us -> 9.97 us  [per_device(): fwd = lax.ppermute(fwd, 'shot', forward)]
    ppermute x3, waiting for transfers between devices: 2.06 us -> 18.9 us  [per_device(): bwd = lax.ppermute(bwd, 'shot', backward)]
    dot_general x8, matrix products: 2.84 us -> 4.69 us  [add(): jnp.einsum('fsk,fkw->fsw', part, rhs, preferred_element_type=jnp.float32)]
    unnamed x15 -> x13, local copies, waits for them, and re-layouts: 4.66 us -> 3.39 us
    ppermute x1, waiting for transfers between devices: 1.23 us -> 0.29 us  [per_device(): first = lax.ppermute(fwd[..., :half], 'shot', forward)]
    ppermute x1, starting transfers between devices: 0.95 us -> 1.86 us  [per_device(): first = lax.ppermute(fwd[..., :half], 'shot', forward)]
    ppermute x1, starting transfers between devices: 1.18 us -> 0.27 us  [per_device(): second = lax.ppermute(bwd[..., half:], 'shot', backward)]
  transfers between devices with their start and end apart: 12 -> 12, of which waited for: 8 -> 6; matrix products, arithmetic and copies ran while one was open for 8% -> 7% of each run, Pallas kernels for 0% -> 0%
where the time goes in v3:
time: 84.4 us; the launch traced here: 84.1 us
  waiting for transfers between devices  43.4 us (51%)
  starting transfers between devices  18.7 us (22%)
  between operations  9.83 us (12%)
  local copies, waits for them, and re-layouts  6.15 us (7%)
  matrix products  5.47 us (6%)
    ppermute x3, waiting for transfers between devices, per_device(): bwd = lax.ppermute(bwd, 'shot', backward)  18.9 us
    all_to_all x1, waiting for transfers between devices, per_device(): pieces = lax.all_to_all(records, 'shot', 2, 0, tiled=True)  10.5 us
    ppermute x3, waiting for transfers between devices, per_device(): fwd = lax.ppermute(fwd, 'shot', forward)  9.97 us
    all_to_all x1, starting transfers between devices, per_device(): pieces = lax.all_to_all(records, 'shot', 2, 0, tiled=True)  7.31 us
    ppermute x3, starting transfers between devices, per_device(): bwd = lax.ppermute(bwd, 'shot', backward)  4.99 us
    dot_general x8, matrix products, add(): jnp.einsum('fsk,fkw->fsw', part, rhs, preferred_element_type=jnp.float32)  4.69 us
    ppermute x1, waiting for transfers between devices, per_device(): second = lax.ppermute(bwd[..., half:], 'shot', backward)  3.72 us
    unnamed x13, local copies, waits for them, and re-layouts  3.39 us
  transfers between devices with their start and end apart: 12, of which 6 were waited for; matrix products, arithmetic and copies ran while one was open for 7% of the time, Pallas kernels for 0%

profile of v3, /device:TPU:0, one launch (start us, length us, event | category | flops | bytes accessed | tf_op | source)
XLA Modules:
  0.0 84.1 jit_solution(12362225092553092673)
XLA Ops:
  0.0 0.0 copy-start
  0.0 0.0 copy-start.2
  0.0 3.4 %copy.40 = bf16[1,2,128,2048]{3,1,0,2:T(2,128)(2,1)} copy(bf16[1,2,128,2048]{3,2,1,0:T(8,128)(2,1)} %param.6) | data formatting | bytes 2097152 | tf_op args[0]
  3.4 7.3 %all-to-all-start = ((bf16[1,2,128,2048]{3,1,0,2:T(2,128)(2,1)}), bf16[1,2,128,2048]{3,1,0,2:T(2,128)(2,1)S(1)}, u32[]{:S(2)}, u32[]{:S(2)}) async-start(bf16[1,2,128,2048]{3,1,0,2:T(2,128)(2,1)} %copy.40), calls=%async_computation | async-start | bytes 2097152 | tf_op jit(solution)/shard_map/all_to_all | solution.py:79
  10.7 0.0 copy-start.3
  10.7 0.0 copy-start.4
  10.7 0.0 copy-start.5
  10.7 0.0 copy-start.1
  10.7 0.0 copy-done
  10.7 0.0 copy-done.2
  10.8 0.8 fusion.13
  11.5 0.1 collective-permute-start
  11.6 1.5 %collective-permute-start.1 = (bf16[1,2,128,512]{2,3,1,0:T(8,128)(2,1)S(1)}, bf16[1,2,128,512]{2,3,1,0:T(8,128)(2,1)S(1)}, u32[]{:S(2)}, u32[]{:S(2)}) collective-permute-start(bf16[1,2,128,512]{2,3,1,0:T(8,128)(2,1)S(1)} %fusion.13), channel_id=1, source_target_pairs={{0,2},{1,3},{2,0},{3,1},{4,6},{5,7},{6,4},{7,5},{8,10},{9,11},{10,... | collective-permute-start | bytes 786440 | tf_op jit(solution)/shard_map/ppermute | solution.py:29
  13.2 1.4 %collective-permute-start.2 = (bf16[1,2,128,512]{2,3,1,0:T(8,128)(2,1)S(1)}, bf16[1,2,128,512]{2,3,1,0:T(8,128)(2,1)S(1)}, u32[]{:S(2)}, u32[]{:S(2)}) collective-permute-start(bf16[1,2,128,512]{2,3,1,0:T(8,128)(2,1)S(1)} %fusion.13), channel_id=1, source_target_pairs={{0,3},{1,0},{2,1},{3,2},{4,7},{5,4},{6,5},{7,6},{8,11},{9,8},{10,9... | collective-permute-start | bytes 786440 | tf_op jit(solution)/shard_map/ppermute | solution.py:29
  14.5 0.0 copy-done.3
  14.6 0.0 copy-done.4
  14.6 0.0 copy-done.5
  14.6 0.7 dynamic_slice.49
  20.2 0.0 copy-done.1
  20.3 0.7 fusion.20
  25.5 0.0 collective-permute-done
  25.5 0.0 collective-permute-done.1
  25.5 0.0 collective-permute-done.2
  25.6 0.2 fusion.17
  25.8 0.1 maximum_maximum_fusion
  25.8 0.1 constant_dynamic-slice_fusion.2
  25.9 10.5 %all-to-all-done = bf16[1,2,128,2048]{3,1,0,2:T(2,128)(2,1)S(1)} async-done(((bf16[1,2,128,2048]{3,1,0,2:T(2,128)(2,1)}), bf16[1,2,128,2048]{3,1,0,2:T(2,128)(2,1)S(1)}, u32[]{:S(2)}, u32[]{:S(2)}) %all-to-all-start) | async-done | bytes 1048608 | tf_op jit(solution)/shard_map/all_to_all | solution.py:79
  36.4 0.4 copy.54
  36.8 0.6 gather_fusion
  37.4 0.1 bitcast_select_fusion
  37.5 0.1 collective-permute-start.3
  37.6 2.0 %collective-permute-start.4 = (bf16[4,1,2,16,2048]{4,3,2,0,1:T(8,128)(2,1)S(1)}, bf16[4,1,2,16,2048]{4,3,2,0,1:T(8,128)(2,1)S(1)}, u32[]{:S(2)}, u32[]{:S(2)}) collective-permute-start(bf16[4,1,2,16,2048]{4,3,2,0,1:T(8,128)(2,1)S(1)} %bitcast_select_fusion), channel_id=1, source_target_pairs={{0,4},{8,0},{16,8},{24,16},{28,24},{20,28},{12,20},{4,12},{1,5},{9... | collective-permute-start | bytes 1572872 | tf_op jit(solution)/shard_map/ppermute | solution.py:96
  39.6 0.1 fusion.41
  39.8 0.5 fusion.21
  40.2 10.0 %collective-permute-done.3 = bf16[4,1,2,16,2048]{4,3,2,0,1:T(8,128)(2,1)S(1)} collective-permute-done((bf16[4,1,2,16,2048]{4,3,2,0,1:T(8,128)(2,1)S(1)}, bf16[4,1,2,16,2048]{4,3,2,0,1:T(8,128)(2,1)S(1)}, u32[]{:S(2)}, u32[]{:S(2)}) %collective-permute-start.3) | collective-permute-done | bytes 524320 | tf_op jit(solution)/shard_map/ppermute | solution.py:93
  50.2 0.0 collective-permute-done.4
  50.3 1.8 %collective-permute-start.6 = (bf16[4,1,2,16,2048]{4,3,2,0,1:T(8,128)(2,1)S(1)}, bf16[4,1,2,16,2048]{4,3,2,0,1:T(8,128)(2,1)S(1)}, u32[]{:S(2)}, u32[]{:S(2)}) collective-permute-start(bf16[4,1,2,16,2048]{4,3,2,0,1:T(8,128)(2,1)S(1)} %collective-permute-done.4), channel_id=1, source_target_pairs={{0,4},{8,0},{16,8},{24,16},{28,24},{20,28},{12,20},{4,12},{1,5},{9... | collective-permute-start | bytes 1572872 | tf_op jit(solution)/shard_map/ppermute | solution.py:96
  52.1 0.3 collective-permute-start.5
  52.4 0.5 convolution_add_fusion.3
  52.8 0.5 convolution_add_fusion.2
  53.3 9.8 %collective-permute-done.6 = bf16[4,1,2,16,2048]{4,3,2,0,1:T(8,128)(2,1)S(1)} collective-permute-done((bf16[4,1,2,16,2048]{4,3,2,0,1:T(8,128)(2,1)S(1)}, bf16[4,1,2,16,2048]{4,3,2,0,1:T(8,128)(2,1)S(1)}, u32[]{:S(2)}, u32[]{:S(2)}) %collective-permute-start.6) | collective-permute-done | bytes 524320 | tf_op jit(solution)/shard_map/ppermute | solution.py:96
  63.1 1.2 %collective-permute-start.8 = (bf16[4,1,2,16,2048]{4,3,2,0,1:T(8,128)(2,1)S(1)}, bf16[4,1,2,16,2048]{4,3,2,0,1:T(8,128)(2,1)S(1)}, u32[]{:S(2)}, u32[]{:S(2)}) collective-permute-start(bf16[4,1,2,16,2048]{4,3,2,0,1:T(8,128)(2,1)S(1)} %collective-permute-done.6), channel_id=1, source_target_pairs={{0,4},{8,0},{16,8},{24,16},{28,24},{20,28},{12,20},{4,12},{1,5},{9... | collective-permute-start | bytes 1572872 | tf_op jit(solution)/shard_map/ppermute | solution.py:96
  64.3 0.0 collective-permute-done.5
  64.3 0.9 %collective-permute-start.7 = (bf16[4,1,2,16,2048]{4,3,2,0,1:T(8,128)(2,1)S(1)}, bf16[4,1,2,16,2048]{4,3,2,0,1:T(8,128)(2,1)S(1)}, u32[]{:S(2)}, u32[]{:S(2)}) collective-permute-start(bf16[4,1,2,16,2048]{4,3,2,0,1:T(8,128)(2,1)S(1)} %collective-permute-done.5), channel_id=1, source_target_pairs={{0,8},{8,16},{16,24},{24,28},{28,20},{20,12},{12,4},{4,0},{1,9},{9... | collective-permute-start | bytes 1572872 | tf_op jit(solution)/shard_map/ppermute | solution.py:93
  65.2 0.5 fusion.22
  65.7 0.5 fusion.6
  66.2 9.1 %collective-permute-done.8 = bf16[4,1,2,16,2048]{4,3,2,0,1:T(8,128)(2,1)S(1)} collective-permute-done((bf16[4,1,2,16,2048]{4,3,2,0,1:T(8,128)(2,1)S(1)}, bf16[4,1,2,16,2048]{4,3,2,0,1:T(8,128)(2,1)S(1)}, u32[]{:S(2)}, u32[]{:S(2)}) %collective-permute-start.8) | collective-permute-done | bytes 524320 | tf_op jit(solution)/shard_map/ppermute | solution.py:96
  75.3 0.3 collective-permute-start.10
  75.6 0.0 collective-permute-done.7
  75.6 1.9 %collective-permute-start.9 = (bf16[4,1,2,16,1024]{4,3,2,0,1:T(8,128)(2,1)S(1)}, bf16[4,1,2,16,1024]{4,3,2,0,1:T(8,128)(2,1)S(1)}, u32[]{:S(2)}, u32[]{:S(2)}) collective-permute-start(bf16[4,1,2,16,1024]{4,3,2,0,1:T(8,128)(2,1)S(1)} %slice.20), channel_id=1, source_target_pairs={{0,8},{8,16},{16,24},{24,28},{28,20},{20,12},{12,4},{4,0},{1,9},{9... | collective-permute-start | bytes 786440 | tf_op jit(solution)/shard_map/ppermute | solution.py:87
  77.6 0.5 fusion.23
  78.0 3.7 %collective-permute-done.10 = bf16[4,1,2,16,1024]{4,3,2,0,1:T(8,128)(2,1)S(1)} collective-permute-done((bf16[4,1,2,16,1024]{4,3,2,0,1:T(8,128)(2,1)S(1)}, bf16[4,1,2,16,1024]{4,3,2,0,1:T(8,128)(2,1)S(1)}, u32[]{:S(2)}, u32[]{:S(2)}) %collective-permute-start.10) | collective-permute-done | bytes 262176 | tf_op jit(solution)/shard_map/ppermute | solution.py:88
  81.7 0.3 collective-permute-done.9
  82.1 0.5 fusion.24
  82.6 1.5 %fusion.7 = bf16[256,2048]{1,0:T(8,128)(2,1)} fusion(f32[256,2048]{1,0:T(8,128)S(1)} %fusion.24, f32[256,2048]{1,0:T(8,128)S(1)} %fusion.23, f32[256,2048]{1,0:T(8,128)S(1)} %fusion.6, bf16[256,128]{0,1:T(8,128)(2,1)S(1)} %bitcast.108, bf16[128,2048]{1,0:T(8,128)(2,1)S(1)} %bitcast.100), kind=kOutput, calls=%fused_computation.12 | convolution fusion | flops 136839168 | bytes 7929856 | tf_op jit(solution)/shard_map/fsk,fkw->fsw/dot_general | solution.py:77
  (20 shorter events, 0.5 us)
Async XLA Ops:
  0.0 10.7 %copy-start = (bf16[1,2,128,2048]{3,2,1,0:T(8,128)(2,1)S(1)}, bf16[1,2,128,2048]{3,2,1,0:T(8,128)(2,1)}, u32[]{:S(2)}) copy-start(bf16[1,2,128,2048]{3,2,1,0:T(8,128)(2,1)} %param.6) | copy-start | bytes 3145732
  0.0 10.7 %copy-start.2 = (s32[4,128]{1,0:T(4,128)S(1)}, s32[4,128]{1,0:T(4,128)}, u32[]{:S(2)}) copy-start(s32[4,128]{1,0:T(4,128)} %param.9) | copy-start | bytes 6148
  3.4 33.1 %all-to-all-start = ((bf16[1,2,128,2048]{3,1,0,2:T(2,128)(2,1)}), bf16[1,2,128,2048]{3,1,0,2:T(2,128)(2,1)S(1)}, u32[]{:S(2)}, u32[]{:S(2)}) async-start(bf16[1,2,128,2048]{3,1,0,2:T(2,128)(2,1)} %copy.40), calls=%async_computation | async-start | bytes 2097152 | tf_op jit(solution)/shard_map/all_to_all | solution.py:79
  10.7 3.9 %copy-start.3 = (s32[128,2]{0,1:T(2,128)S(1)}, s32[128,2]{0,1:T(2,128)}, u32[]{:S(2)}) copy-start(s32[128,2]{0,1:T(2,128)} %param.7) | copy-start | bytes 3076
  10.7 3.9 %copy-start.4 = (s32[4]{0:T(128)S(1)}, s32[4]{0:T(128)}, u32[]{:S(2)}) copy-start(s32[4]{0:T(128)} %param.8) | copy-start | bytes 52
  10.7 3.9 %copy-start.5 = (s32[8]{0:T(128)S(1)}, s32[8]{0:T(128)}, u32[]{:S(2)}) copy-start(s32[8]{0:T(128)} %constant.105.clone) | copy-start | bytes 100
  10.7 9.5 %copy-start.1 = (s32[8]{0:T(128)S(1)}, s32[8]{0:T(128)}, u32[]{:S(2)}) copy-start(s32[8]{0:T(128)} %constant.104.clone) | copy-start | bytes 100
  11.5 14.0 %collective-permute-start = (bf16[1,2,128,512]{2,3,1,0:T(8,128)(2,1)S(1)}, bf16[1,2,128,512]{2,3,1,0:T(8,128)(2,1)S(1)}, u32[]{:S(2)}, u32[]{:S(2)}) collective-permute-start(bf16[1,2,128,512]{2,3,1,0:T(8,128)(2,1)S(1)} %fusion.13), channel_id=1, source_target_pairs={{0,1},{1,2},{2,3},{3,0},{4,5},{5,6},{6,7},{7,4},{8,9},{9,10},{10,1... | collective-permute-start | bytes 786440 | tf_op jit(solution)/shard_map/ppermute | solution.py:29
  11.6 13.9 %collective-permute-start.1 = (bf16[1,2,128,512]{2,3,1,0:T(8,128)(2,1)S(1)}, bf16[1,2,128,512]{2,3,1,0:T(8,128)(2,1)S(1)}, u32[]{:S(2)}, u32[]{:S(2)}) collective-permute-start(bf16[1,2,128,512]{2,3,1,0:T(8,128)(2,1)S(1)} %fusion.13), channel_id=1, source_target_pairs={{0,2},{1,3},{2,0},{3,1},{4,6},{5,7},{6,4},{7,5},{8,10},{9,11},{10,... | collective-permute-start | bytes 786440 | tf_op jit(solution)/shard_map/ppermute | solution.py:29
  13.2 12.4 %collective-permute-start.2 = (bf16[1,2,128,512]{2,3,1,0:T(8,128)(2,1)S(1)}, bf16[1,2,128,512]{2,3,1,0:T(8,128)(2,1)S(1)}, u32[]{:S(2)}, u32[]{:S(2)}) collective-permute-start(bf16[1,2,128,512]{2,3,1,0:T(8,128)(2,1)S(1)} %fusion.13), channel_id=1, source_target_pairs={{0,3},{1,0},{2,1},{3,2},{4,7},{5,4},{6,5},{7,6},{8,11},{9,8},{10,9... | collective-permute-start | bytes 786440 | tf_op jit(solution)/shard_map/ppermute | solution.py:29
  37.5 12.7 %collective-permute-start.3 = (bf16[4,1,2,16,2048]{4,3,2,0,1:T(8,128)(2,1)S(1)}, bf16[4,1,2,16,2048]{4,3,2,0,1:T(8,128)(2,1)S(1)}, u32[]{:S(2)}, u32[]{:S(2)}) collective-permute-start(bf16[4,1,2,16,2048]{4,3,2,0,1:T(8,128)(2,1)S(1)} %bitcast_select_fusion), channel_id=1, source_target_pairs={{0,8},{8,16},{16,24},{24,28},{28,20},{20,12},{12,4},{4,0},{1,9},{9... | collective-permute-start | bytes 1572872 | tf_op jit(solution)/shard_map/ppermute | solution.py:93
  37.6 12.7 %collective-permute-start.4 = (bf16[4,1,2,16,2048]{4,3,2,0,1:T(8,128)(2,1)S(1)}, bf16[4,1,2,16,2048]{4,3,2,0,1:T(8,128)(2,1)S(1)}, u32[]{:S(2)}, u32[]{:S(2)}) collective-permute-start(bf16[4,1,2,16,2048]{4,3,2,0,1:T(8,128)(2,1)S(1)} %bitcast_select_fusion), channel_id=1, source_target_pairs={{0,4},{8,0},{16,8},{24,16},{28,24},{20,28},{12,20},{4,12},{1,5},{9... | collective-permute-start | bytes 1572872 | tf_op jit(solution)/shard_map/ppermute | solution.py:96
  50.3 12.8 %collective-permute-start.6 = (bf16[4,1,2,16,2048]{4,3,2,0,1:T(8,128)(2,1)S(1)}, bf16[4,1,2,16,2048]{4,3,2,0,1:T(8,128)(2,1)S(1)}, u32[]{:S(2)}, u32[]{:S(2)}) collective-permute-start(bf16[4,1,2,16,2048]{4,3,2,0,1:T(8,128)(2,1)S(1)} %collective-permute-done.4), channel_id=1, source_target_pairs={{0,4},{8,0},{16,8},{24,16},{28,24},{20,28},{12,20},{4,12},{1,5},{9... | collective-permute-start | bytes 1572872 | tf_op jit(solution)/shard_map/ppermute | solution.py:96
  52.1 12.2 %collective-permute-start.5 = (bf16[4,1,2,16,2048]{4,3,2,0,1:T(8,128)(2,1)S(1)}, bf16[4,1,2,16,2048]{4,3,2,0,1:T(8,128)(2,1)S(1)}, u32[]{:S(2)}, u32[]{:S(2)}) collective-permute-start(bf16[4,1,2,16,2048]{4,3,2,0,1:T(8,128)(2,1)S(1)} %collective-permute-done.3), channel_id=1, source_target_pairs={{0,8},{8,16},{16,24},{24,28},{28,20},{20,12},{12,4},{4,0},{1,9},{9... | collective-permute-start | bytes 1572872 | tf_op jit(solution)/shard_map/ppermute | solution.py:93
  63.1 12.2 %collective-permute-start.8 = (bf16[4,1,2,16,2048]{4,3,2,0,1:T(8,128)(2,1)S(1)}, bf16[4,1,2,16,2048]{4,3,2,0,1:T(8,128)(2,1)S(1)}, u32[]{:S(2)}, u32[]{:S(2)}) collective-permute-start(bf16[4,1,2,16,2048]{4,3,2,0,1:T(8,128)(2,1)S(1)} %collective-permute-done.6), channel_id=1, source_target_pairs={{0,4},{8,0},{16,8},{24,16},{28,24},{20,28},{12,20},{4,12},{1,5},{9... | collective-permute-start | bytes 1572872 | tf_op jit(solution)/shard_map/ppermute | solution.py:96
  64.3 11.3 %collective-permute-start.7 = (bf16[4,1,2,16,2048]{4,3,2,0,1:T(8,128)(2,1)S(1)}, bf16[4,1,2,16,2048]{4,3,2,0,1:T(8,128)(2,1)S(1)}, u32[]{:S(2)}, u32[]{:S(2)}) collective-permute-start(bf16[4,1,2,16,2048]{4,3,2,0,1:T(8,128)(2,1)S(1)} %collective-permute-done.5), channel_id=1, source_target_pairs={{0,8},{8,16},{16,24},{24,28},{28,20},{20,12},{12,4},{4,0},{1,9},{9... | collective-permute-start | bytes 1572872 | tf_op jit(solution)/shard_map/ppermute | solution.py:93
  75.3 6.4 %collective-permute-start.10 = (bf16[4,1,2,16,1024]{4,3,2,0,1:T(8,128)(2,1)S(1)}, bf16[4,1,2,16,1024]{4,3,2,0,1:T(8,128)(2,1)S(1)}, u32[]{:S(2)}, u32[]{:S(2)}) collective-permute-start(bf16[4,1,2,16,1024]{4,3,2,0,1:T(8,128)(2,1)S(1)} %slice.21), channel_id=1, source_target_pairs={{0,4},{8,0},{16,8},{24,16},{28,24},{20,28},{12,20},{4,12},{1,5},{9... | collective-permute-start | bytes 786440 | tf_op jit(solution)/shard_map/ppermute | solution.py:88
  75.6 6.4 %collective-permute-start.9 = (bf16[4,1,2,16,1024]{4,3,2,0,1:T(8,128)(2,1)S(1)}, bf16[4,1,2,16,1024]{4,3,2,0,1:T(8,128)(2,1)S(1)}, u32[]{:S(2)}, u32[]{:S(2)}) collective-permute-start(bf16[4,1,2,16,1024]{4,3,2,0,1:T(8,128)(2,1)S(1)} %slice.20), channel_id=1, source_target_pairs={{0,8},{8,16},{16,24},{24,28},{28,20},{20,12},{12,4},{4,0},{1,9},{9... | collective-permute-start | bytes 786440 | tf_op jit(solution)/shard_map/ppermute | solution.py:87

commit v4 on v3

--- a/solution.py
+++ b/solution.py
@@ -76,8 +76,8 @@
         rhs = piece.transpose(1, 2, 0, 3, 4).reshape(freqs, -1, rcv_here)
         return total + jnp.einsum("fsk,fkw->fsw", part, rhs, preferred_element_type=jnp.float32)
 
-    pieces = lax.all_to_all(records, "shot", 2, 0, tiled=True)
-    pieces = pieces.reshape(n_shot, freqs, parts, rows, rcv_here)
+    split = records.reshape(freqs, parts, n_shot, rows, rcv_here).transpose(2, 0, 1, 3, 4)
+    pieces = lax.all_to_all(split, "shot", 0, 0, tiled=True)
     mine = jnp.take(pieces, block_owner, axis=0)
 
     total = add(jnp.zeros((freqs, 2 * shots_here, rcv_here), jnp.float32), mine, me)

time: 84.4 us -> 83.1 us (0.985)
  local copies, waits for them, and re-layouts: 6.15 us -> 4.81 us
    unnamed x13 -> x12, local copies, waits for them, and re-layouts: 3.39 us -> 0.03 us
    transpose x0 -> x1, local copies, waits for them, and re-layouts: none -> 2.39 us  [per_device(): records.reshape(freqs, parts, n_shot, rows, rcv_here)]
where the time goes in v4:
time: 83.1 us; the launch traced here: 82.7 us
  waiting for transfers between devices  43.4 us (52%)
  starting transfers between devices  18.7 us (23%)
  between operations  9.82 us (12%)
  matrix products  5.46 us (7%)
  local copies, waits for them, and re-layouts  4.81 us (6%)
    ppermute x3, waiting for transfers between devices, per_device(): bwd = lax.ppermute(bwd, 'shot', backward)  18.9 us
    all_to_all x1, waiting for transfers between devices, per_device(): pieces = lax.all_to_all(split, 'shot', 0, 0, tiled=True)  10.5 us
    ppermute x3, waiting for transfers between devices, per_device(): fwd = lax.ppermute(fwd, 'shot', forward)  9.98 us
    all_to_all x1, starting transfers between devices, per_device(): pieces = lax.all_to_all(split, 'shot', 0, 0, tiled=True)  7.31 us
    ppermute x3, starting transfers between devices, per_device(): bwd = lax.ppermute(bwd, 'shot', backward)  4.99 us
    dot_general x8, matrix products, add(): jnp.einsum('fsk,fkw->fsw', part, rhs, preferred_element_type=jnp.float32)  4.68 us
    ppermute x1, waiting for transfers between devices, per_device(): second = lax.ppermute(bwd[..., half:], 'shot', backward)  3.73 us
    ppermute x3, starting transfers between devices, gather_near(): lax.ppermute(picked, 'rcv', [(i, (i + k) % n_rcv) for i in range(n_rcv)])  3 us
  transfers between devices with their start and end apart: 12, of which 6 were waited for; matrix products, arithmetic and copies ran while one was open for 7% of the time, Pallas kernels for 0%

profile of v4, /device:TPU:0, one launch (start us, length us, event | category | flops | bytes accessed | tf_op | source)
XLA Modules:
  0.0 82.7 jit_solution(6761190764548943430)
XLA Ops:
  0.0 0.0 copy-start
  0.0 0.0 copy-start.2
  0.0 2.4 %copy.38 = bf16[8,1,2,16,2048]{4,3,2,1,0:T(8,128)(2,1)} copy(bf16[8,1,2,16,2048]{4,3,0,2,1:T(8,128)(2,1)} %bitcast.100) | data formatting | bytes 2097152 | tf_op jit(solution)/shard_map/transpose | solution.py:79
  2.4 7.3 %all-to-all-start = ((bf16[8,1,2,16,2048]{4,3,2,1,0:T(8,128)(2,1)}), bf16[8,1,2,16,2048]{4,3,2,1,0:T(8,128)(2,1)S(1)}, u32[]{:S(2)}, u32[]{:S(2)}) async-start(bf16[8,1,2,16,2048]{4,3,2,1,0:T(8,128)(2,1)} %copy.38), calls=%async_computation | async-start | bytes 2097152 | tf_op jit(solution)/shard_map/all_to_all | solution.py:80
  9.7 0.0 copy-start.3
  9.7 0.0 copy-start.4
  9.7 0.0 copy-start.5
  9.7 0.0 copy-start.1
  9.8 0.0 copy-done
  9.8 0.0 copy-done.2
  9.8 0.8 fusion.13
  10.6 0.1 collective-permute-start
  10.6 1.6 %collective-permute-start.1 = (bf16[1,2,128,512]{2,3,1,0:T(8,128)(2,1)S(1)}, bf16[1,2,128,512]{2,3,1,0:T(8,128)(2,1)S(1)}, u32[]{:S(2)}, u32[]{:S(2)}) collective-permute-start(bf16[1,2,128,512]{2,3,1,0:T(8,128)(2,1)S(1)} %fusion.13), channel_id=1, source_target_pairs={{0,2},{1,3},{2,0},{3,1},{4,6},{5,7},{6,4},{7,5},{8,10},{9,11},{10,... | collective-permute-start | bytes 786440 | tf_op jit(solution)/shard_map/ppermute | solution.py:29
  12.2 1.4 %collective-permute-start.2 = (bf16[1,2,128,512]{2,3,1,0:T(8,128)(2,1)S(1)}, bf16[1,2,128,512]{2,3,1,0:T(8,128)(2,1)S(1)}, u32[]{:S(2)}, u32[]{:S(2)}) collective-permute-start(bf16[1,2,128,512]{2,3,1,0:T(8,128)(2,1)S(1)} %fusion.13), channel_id=1, source_target_pairs={{0,3},{1,0},{2,1},{3,2},{4,7},{5,4},{6,5},{7,6},{8,11},{9,8},{10,9... | collective-permute-start | bytes 786440 | tf_op jit(solution)/shard_map/ppermute | solution.py:29
  13.6 0.0 copy-done.3
  13.6 0.0 copy-done.4
  13.6 0.0 copy-done.5
  13.6 0.7 dynamic_slice.49
  19.3 0.0 copy-done.1
  19.3 0.7 fusion.20
  24.5 0.0 collective-permute-done
  24.5 0.0 collective-permute-done.1
  24.5 0.0 collective-permute-done.2
  24.6 0.2 fusion.17
  24.8 0.1 maximum_maximum_fusion
  24.9 0.1 constant_dynamic-slice_fusion.2
  24.9 10.5 %all-to-all-done = bf16[8,1,2,16,2048]{4,3,2,1,0:T(8,128)(2,1)S(1)} async-done(((bf16[8,1,2,16,2048]{4,3,2,1,0:T(8,128)(2,1)}), bf16[8,1,2,16,2048]{4,3,2,1,0:T(8,128)(2,1)S(1)}, u32[]{:S(2)}, u32[]{:S(2)}) %all-to-all-start) | async-done | bytes 1048608 | tf_op jit(solution)/shard_map/all_to_all | solution.py:80
  35.5 0.6 gather_fusion
  36.1 0.1 bitcast_select_fusion
  36.2 0.1 collective-permute-start.3
  36.2 2.0 %collective-permute-start.4 = (bf16[4,1,2,16,2048]{4,3,2,0,1:T(8,128)(2,1)S(1)}, bf16[4,1,2,16,2048]{4,3,2,0,1:T(8,128)(2,1)S(1)}, u32[]{:S(2)}, u32[]{:S(2)}) collective-permute-start(bf16[4,1,2,16,2048]{4,3,2,0,1:T(8,128)(2,1)S(1)} %bitcast_select_fusion), channel_id=1, source_target_pairs={{0,4},{8,0},{16,8},{24,16},{28,24},{20,28},{12,20},{4,12},{1,5},{9... | collective-permute-start | bytes 1572872 | tf_op jit(solution)/shard_map/ppermute | solution.py:96
  38.3 0.1 fusion.41
  38.4 0.5 fusion.21
  38.9 10.0 %collective-permute-done.3 = bf16[4,1,2,16,2048]{4,3,2,0,1:T(8,128)(2,1)S(1)} collective-permute-done((bf16[4,1,2,16,2048]{4,3,2,0,1:T(8,128)(2,1)S(1)}, bf16[4,1,2,16,2048]{4,3,2,0,1:T(8,128)(2,1)S(1)}, u32[]{:S(2)}, u32[]{:S(2)}) %collective-permute-start.3) | collective-permute-done | bytes 524320 | tf_op jit(solution)/shard_map/ppermute | solution.py:93
  48.9 0.0 collective-permute-done.4
  49.0 1.8 %collective-permute-start.6 = (bf16[4,1,2,16,2048]{4,3,2,0,1:T(8,128)(2,1)S(1)}, bf16[4,1,2,16,2048]{4,3,2,0,1:T(8,128)(2,1)S(1)}, u32[]{:S(2)}, u32[]{:S(2)}) collective-permute-start(bf16[4,1,2,16,2048]{4,3,2,0,1:T(8,128)(2,1)S(1)} %collective-permute-done.4), channel_id=1, source_target_pairs={{0,4},{8,0},{16,8},{24,16},{28,24},{20,28},{12,20},{4,12},{1,5},{9... | collective-permute-start | bytes 1572872 | tf_op jit(solution)/shard_map/ppermute | solution.py:96
  50.8 0.3 collective-permute-start.5
  51.0 0.5 convolution_add_fusion.3
  51.5 0.5 convolution_add_fusion.2
  52.0 9.8 %collective-permute-done.6 = bf16[4,1,2,16,2048]{4,3,2,0,1:T(8,128)(2,1)S(1)} collective-permute-done((bf16[4,1,2,16,2048]{4,3,2,0,1:T(8,128)(2,1)S(1)}, bf16[4,1,2,16,2048]{4,3,2,0,1:T(8,128)(2,1)S(1)}, u32[]{:S(2)}, u32[]{:S(2)}) %collective-permute-start.6) | collective-permute-done | bytes 524320 | tf_op jit(solution)/shard_map/ppermute | solution.py:96
  61.8 1.2 %collective-permute-start.8 = (bf16[4,1,2,16,2048]{4,3,2,0,1:T(8,128)(2,1)S(1)}, bf16[4,1,2,16,2048]{4,3,2,0,1:T(8,128)(2,1)S(1)}, u32[]{:S(2)}, u32[]{:S(2)}) collective-permute-start(bf16[4,1,2,16,2048]{4,3,2,0,1:T(8,128)(2,1)S(1)} %collective-permute-done.6), channel_id=1, source_target_pairs={{0,4},{8,0},{16,8},{24,16},{28,24},{20,28},{12,20},{4,12},{1,5},{9... | collective-permute-start | bytes 1572872 | tf_op jit(solution)/shard_map/ppermute | solution.py:96
  62.9 0.0 collective-permute-done.5
  62.9 0.9 %collective-permute-start.7 = (bf16[4,1,2,16,2048]{4,3,2,0,1:T(8,128)(2,1)S(1)}, bf16[4,1,2,16,2048]{4,3,2,0,1:T(8,128)(2,1)S(1)}, u32[]{:S(2)}, u32[]{:S(2)}) collective-permute-start(bf16[4,1,2,16,2048]{4,3,2,0,1:T(8,128)(2,1)S(1)} %collective-permute-done.5), channel_id=1, source_target_pairs={{0,8},{8,16},{16,24},{24,28},{28,20},{20,12},{12,4},{4,0},{1,9},{9... | collective-permute-start | bytes 1572872 | tf_op jit(solution)/shard_map/ppermute | solution.py:93
  63.8 0.5 fusion.22
  64.3 0.5 fusion.6
  64.8 9.1 %collective-permute-done.8 = bf16[4,1,2,16,2048]{4,3,2,0,1:T(8,128)(2,1)S(1)} collective-permute-done((bf16[4,1,2,16,2048]{4,3,2,0,1:T(8,128)(2,1)S(1)}, bf16[4,1,2,16,2048]{4,3,2,0,1:T(8,128)(2,1)S(1)}, u32[]{:S(2)}, u32[]{:S(2)}) %collective-permute-start.8) | collective-permute-done | bytes 524320 | tf_op jit(solution)/shard_map/ppermute | solution.py:96
  74.0 0.3 collective-permute-start.10
  74.2 0.0 collective-permute-done.7
  74.3 1.9 %collective-permute-start.9 = (bf16[4,1,2,16,1024]{4,3,2,0,1:T(8,128)(2,1)S(1)}, bf16[4,1,2,16,1024]{4,3,2,0,1:T(8,128)(2,1)S(1)}, u32[]{:S(2)}, u32[]{:S(2)}) collective-permute-start(bf16[4,1,2,16,1024]{4,3,2,0,1:T(8,128)(2,1)S(1)} %slice.20), channel_id=1, source_target_pairs={{0,8},{8,16},{16,24},{24,28},{28,20},{20,12},{12,4},{4,0},{1,9},{9... | collective-permute-start | bytes 786440 | tf_op jit(solution)/shard_map/ppermute | solution.py:87
  76.2 0.5 fusion.23
  76.7 3.7 %collective-permute-done.10 = bf16[4,1,2,16,1024]{4,3,2,0,1:T(8,128)(2,1)S(1)} collective-permute-done((bf16[4,1,2,16,1024]{4,3,2,0,1:T(8,128)(2,1)S(1)}, bf16[4,1,2,16,1024]{4,3,2,0,1:T(8,128)(2,1)S(1)}, u32[]{:S(2)}, u32[]{:S(2)}) %collective-permute-start.10) | collective-permute-done | bytes 262176 | tf_op jit(solution)/shard_map/ppermute | solution.py:88
  80.4 0.3 collective-permute-done.9
  80.8 0.5 fusion.24
  81.2 1.5 %fusion.7 = bf16[256,2048]{1,0:T(8,128)(2,1)} fusion(f32[256,2048]{1,0:T(8,128)S(1)} %fusion.24, f32[256,2048]{1,0:T(8,128)S(1)} %fusion.23, f32[256,2048]{1,0:T(8,128)S(1)} %fusion.6, bf16[256,128]{0,1:T(8,128)(2,1)S(1)} %bitcast.106, bf16[128,2048]{1,0:T(8,128)(2,1)S(1)} %bitcast.97), kind=kOutput, calls=%fused_computation.12 | convolution fusion | flops 136839168 | bytes 7929856 | tf_op jit(solution)/shard_map/fsk,fkw->fsw/dot_general | solution.py:77
  (20 shorter events, 0.5 us)
Async XLA Ops:
  0.0 9.8 %copy-start = (bf16[1,2,128,2048]{3,2,1,0:T(8,128)(2,1)S(1)}, bf16[1,2,128,2048]{3,2,1,0:T(8,128)(2,1)}, u32[]{:S(2)}) copy-start(bf16[1,2,128,2048]{3,2,1,0:T(8,128)(2,1)} %param.6) | copy-start | bytes 3145732
  0.0 9.8 %copy-start.2 = (s32[4,128]{1,0:T(4,128)S(1)}, s32[4,128]{1,0:T(4,128)}, u32[]{:S(2)}) copy-start(s32[4,128]{1,0:T(4,128)} %param.9) | copy-start | bytes 6148
  2.4 33.1 %all-to-all-start = ((bf16[8,1,2,16,2048]{4,3,2,1,0:T(8,128)(2,1)}), bf16[8,1,2,16,2048]{4,3,2,1,0:T(8,128)(2,1)S(1)}, u32[]{:S(2)}, u32[]{:S(2)}) async-start(bf16[8,1,2,16,2048]{4,3,2,1,0:T(8,128)(2,1)} %copy.38), calls=%async_computation | async-start | bytes 2097152 | tf_op jit(solution)/shard_map/all_to_all | solution.py:80
  9.7 3.9 %copy-start.3 = (s32[128,2]{0,1:T(2,128)S(1)}, s32[128,2]{0,1:T(2,128)}, u32[]{:S(2)}) copy-start(s32[128,2]{0,1:T(2,128)} %param.7) | copy-start | bytes 3076
  9.7 3.9 %copy-start.4 = (s32[4]{0:T(128)S(1)}, s32[4]{0:T(128)}, u32[]{:S(2)}) copy-start(s32[4]{0:T(128)} %param.8) | copy-start | bytes 52
  9.7 3.9 %copy-start.5 = (s32[8]{0:T(128)S(1)}, s32[8]{0:T(128)}, u32[]{:S(2)}) copy-start(s32[8]{0:T(128)} %constant.105.clone) | copy-start | bytes 100
  9.7 9.5 %copy-start.1 = (s32[8]{0:T(128)S(1)}, s32[8]{0:T(128)}, u32[]{:S(2)}) copy-start(s32[8]{0:T(128)} %constant.104.clone) | copy-start | bytes 100
  10.6 14.0 %collective-permute-start = (bf16[1,2,128,512]{2,3,1,0:T(8,128)(2,1)S(1)}, bf16[1,2,128,512]{2,3,1,0:T(8,128)(2,1)S(1)}, u32[]{:S(2)}, u32[]{:S(2)}) collective-permute-start(bf16[1,2,128,512]{2,3,1,0:T(8,128)(2,1)S(1)} %fusion.13), channel_id=1, source_target_pairs={{0,1},{1,2},{2,3},{3,0},{4,5},{5,6},{6,7},{7,4},{8,9},{9,10},{10,1... | collective-permute-start | bytes 786440 | tf_op jit(solution)/shard_map/ppermute | solution.py:29
  10.6 13.9 %collective-permute-start.1 = (bf16[1,2,128,512]{2,3,1,0:T(8,128)(2,1)S(1)}, bf16[1,2,128,512]{2,3,1,0:T(8,128)(2,1)S(1)}, u32[]{:S(2)}, u32[]{:S(2)}) collective-permute-start(bf16[1,2,128,512]{2,3,1,0:T(8,128)(2,1)S(1)} %fusion.13), channel_id=1, source_target_pairs={{0,2},{1,3},{2,0},{3,1},{4,6},{5,7},{6,4},{7,5},{8,10},{9,11},{10,... | collective-permute-start | bytes 786440 | tf_op jit(solution)/shard_map/ppermute | solution.py:29
  12.2 12.4 %collective-permute-start.2 = (bf16[1,2,128,512]{2,3,1,0:T(8,128)(2,1)S(1)}, bf16[1,2,128,512]{2,3,1,0:T(8,128)(2,1)S(1)}, u32[]{:S(2)}, u32[]{:S(2)}) collective-permute-start(bf16[1,2,128,512]{2,3,1,0:T(8,128)(2,1)S(1)} %fusion.13), channel_id=1, source_target_pairs={{0,3},{1,0},{2,1},{3,2},{4,7},{5,4},{6,5},{7,6},{8,11},{9,8},{10,9... | collective-permute-start | bytes 786440 | tf_op jit(solution)/shard_map/ppermute | solution.py:29
  36.2 12.7 %collective-permute-start.3 = (bf16[4,1,2,16,2048]{4,3,2,0,1:T(8,128)(2,1)S(1)}, bf16[4,1,2,16,2048]{4,3,2,0,1:T(8,128)(2,1)S(1)}, u32[]{:S(2)}, u32[]{:S(2)}) collective-permute-start(bf16[4,1,2,16,2048]{4,3,2,0,1:T(8,128)(2,1)S(1)} %bitcast_select_fusion), channel_id=1, source_target_pairs={{0,8},{8,16},{16,24},{24,28},{28,20},{20,12},{12,4},{4,0},{1,9},{9... | collective-permute-start | bytes 1572872 | tf_op jit(solution)/shard_map/ppermute | solution.py:93
  36.2 12.7 %collective-permute-start.4 = (bf16[4,1,2,16,2048]{4,3,2,0,1:T(8,128)(2,1)S(1)}, bf16[4,1,2,16,2048]{4,3,2,0,1:T(8,128)(2,1)S(1)}, u32[]{:S(2)}, u32[]{:S(2)}) collective-permute-start(bf16[4,1,2,16,2048]{4,3,2,0,1:T(8,128)(2,1)S(1)} %bitcast_select_fusion), channel_id=1, source_target_pairs={{0,4},{8,0},{16,8},{24,16},{28,24},{20,28},{12,20},{4,12},{1,5},{9... | collective-permute-start | bytes 1572872 | tf_op jit(solution)/shard_map/ppermute | solution.py:96
  49.0 12.8 %collective-permute-start.6 = (bf16[4,1,2,16,2048]{4,3,2,0,1:T(8,128)(2,1)S(1)}, bf16[4,1,2,16,2048]{4,3,2,0,1:T(8,128)(2,1)S(1)}, u32[]{:S(2)}, u32[]{:S(2)}) collective-permute-start(bf16[4,1,2,16,2048]{4,3,2,0,1:T(8,128)(2,1)S(1)} %collective-permute-done.4), channel_id=1, source_target_pairs={{0,4},{8,0},{16,8},{24,16},{28,24},{20,28},{12,20},{4,12},{1,5},{9... | collective-permute-start | bytes 1572872 | tf_op jit(solution)/shard_map/ppermute | solution.py:96
  50.8 12.2 %collective-permute-start.5 = (bf16[4,1,2,16,2048]{4,3,2,0,1:T(8,128)(2,1)S(1)}, bf16[4,1,2,16,2048]{4,3,2,0,1:T(8,128)(2,1)S(1)}, u32[]{:S(2)}, u32[]{:S(2)}) collective-permute-start(bf16[4,1,2,16,2048]{4,3,2,0,1:T(8,128)(2,1)S(1)} %collective-permute-done.3), channel_id=1, source_target_pairs={{0,8},{8,16},{16,24},{24,28},{28,20},{20,12},{12,4},{4,0},{1,9},{9... | collective-permute-start | bytes 1572872 | tf_op jit(solution)/shard_map/ppermute | solution.py:93
  61.8 12.2 %collective-permute-start.8 = (bf16[4,1,2,16,2048]{4,3,2,0,1:T(8,128)(2,1)S(1)}, bf16[4,1,2,16,2048]{4,3,2,0,1:T(8,128)(2,1)S(1)}, u32[]{:S(2)}, u32[]{:S(2)}) collective-permute-start(bf16[4,1,2,16,2048]{4,3,2,0,1:T(8,128)(2,1)S(1)} %collective-permute-done.6), channel_id=1, source_target_pairs={{0,4},{8,0},{16,8},{24,16},{28,24},{20,28},{12,20},{4,12},{1,5},{9... | collective-permute-start | bytes 1572872 | tf_op jit(solution)/shard_map/ppermute | solution.py:96
  62.9 11.3 %collective-permute-start.7 = (bf16[4,1,2,16,2048]{4,3,2,0,1:T(8,128)(2,1)S(1)}, bf16[4,1,2,16,2048]{4,3,2,0,1:T(8,128)(2,1)S(1)}, u32[]{:S(2)}, u32[]{:S(2)}) collective-permute-start(bf16[4,1,2,16,2048]{4,3,2,0,1:T(8,128)(2,1)S(1)} %collective-permute-done.5), channel_id=1, source_target_pairs={{0,8},{8,16},{16,24},{24,28},{28,20},{20,12},{12,4},{4,0},{1,9},{9... | collective-permute-start | bytes 1572872 | tf_op jit(solution)/shard_map/ppermute | solution.py:93
  74.0 6.4 %collective-permute-start.10 = (bf16[4,1,2,16,1024]{4,3,2,0,1:T(8,128)(2,1)S(1)}, bf16[4,1,2,16,1024]{4,3,2,0,1:T(8,128)(2,1)S(1)}, u32[]{:S(2)}, u32[]{:S(2)}) collective-permute-start(bf16[4,1,2,16,1024]{4,3,2,0,1:T(8,128)(2,1)S(1)} %slice.21), channel_id=1, source_target_pairs={{0,4},{8,0},{16,8},{24,16},{28,24},{20,28},{12,20},{4,12},{1,5},{9... | collective-permute-start | bytes 786440 | tf_op jit(solution)/shard_map/ppermute | solution.py:88
  74.3 6.4 %collective-permute-start.9 = (bf16[4,1,2,16,1024]{4,3,2,0,1:T(8,128)(2,1)S(1)}, bf16[4,1,2,16,1024]{4,3,2,0,1:T(8,128)(2,1)S(1)}, u32[]{:S(2)}, u32[]{:S(2)}) collective-permute-start(bf16[4,1,2,16,1024]{4,3,2,0,1:T(8,128)(2,1)S(1)} %slice.20), channel_id=1, source_target_pairs={{0,8},{8,16},{16,24},{24,28},{28,20},{20,12},{12,4},{4,0},{1,9},{9... | collective-permute-start | bytes 786440 | tf_op jit(solution)/shard_map/ppermute | solution.py:87
